TPU v7x, 256 devices: a whole 4x4x8 slice. The times are simulated.
256 devices in a mesh: ctx: 32 (over y, z), rep: 8 (over x, core).
Axes of the slice: x: 4, y: 4, z: 8, core: 2. Of those that a mesh axis runs over, the one named last changes fastest.
Arguments:
- queries: bfloat16 [32768, 4096], P(('rep', 'ctx')), parts along dimension 0, may hold values from -6 to 6
- key_rows: bfloat16 [32768, 4096], P(('rep', 'ctx')), parts along dimension 0, may hold values from -6 to 6
- value_rows: bfloat16 [32768, 4096], P(('rep', 'ctx')), parts along dimension 0, may hold values from -8 to 8
- doc_blocks: int32 [24], P('rep'), parts along dimension 0, may hold values from 1 to 16, 32 in all
- phm_mix: float32 [4, 4, 4], replicated, may hold values from -4 to 4
- phm_blocks: bfloat16 [4096, 1280], P('ctx'), may hold values from -0.09375 to 0.09375
Outputs:
- projected: bfloat16 [32768, 5120], P(('rep', 'ctx')), parts along dimension 0
There are 8 independent parts, one for each index of `rep`. A program takes and returns all parts, laid end to end along the dimension named above; an argument that names none is the same for every part. Nothing has to cross between parts.
Inputs may be any that keep to these rules, and one draw needn't show every extreme that they name: `doc_blocks`: entries sum to 32; the largest entry is exactly 16.
All inputs are finite; a program needn't handle non-finite values.
Results may differ from a plain program's by a relative error of at most 0.006.
Values may be sent and summed in bfloat16 or wider, within the bound.
No kernel may reach another device: no remote copies, remote signals or barrier semaphores. Data moves between devices by JAX's collectives and lax.ppermute only.
A program may use at most 64 MiB of HBM per device.

v0:
```python
import math

import jax
import jax.numpy as jnp
from jax import lax
from jax.sharding import PartitionSpec as P

HEAD_DIM = 128
PHM_N = 4
UNIT = 128


def attend(q_all, k_all, v_all, doc_ids):
    seq_len = q_all.shape[0]
    block = min(512, seq_len)
    count = seq_len // block
    scale = 1.0 / math.sqrt(HEAD_DIM)
    heads_here = q_all.shape[1]

    def query_block(which):
        anchor = which * block
        q_part = lax.dynamic_slice_in_dim(q_all, anchor, block, 0)
        q_docs = lax.dynamic_slice_in_dim(doc_ids, anchor, block, 0)
        q_pos = anchor + jnp.arange(block, dtype=jnp.int32)
        lowest = jnp.int32(0)

        def key_block(kb, carry):
            running, total, accum = carry
            k_part = lax.dynamic_slice_in_dim(k_all, kb * block, block, 0)
            v_part = lax.dynamic_slice_in_dim(v_all, kb * block, block, 0)
            k_docs = lax.dynamic_slice_in_dim(doc_ids, kb * block, block, 0)
            k_pos = kb * block + jnp.arange(block, dtype=jnp.int32)
            allowed = (k_pos[None, :] <= q_pos[:, None]) & (k_docs[None, :] == q_docs[:, None])
            scores = (
                jnp.einsum("qhe,khe->hqk", q_part, k_part, preferred_element_type=jnp.float32)
                * scale
            )
            scores = jnp.where(allowed[None], scores, -1e30)
            newest = jnp.maximum(running, jnp.max(scores, axis=2))
            factor = jnp.exp(running - newest)
            expd = jnp.where(allowed[None], jnp.exp(scores - newest[:, :, None]), 0.0)
            total = total * factor + jnp.sum(expd, axis=2)
            update = jnp.einsum(
                "hqk,khe->hqe",
                expd.astype(jnp.bfloat16),
                v_part,
                preferred_element_type=jnp.float32,
            )
            accum = accum * factor[:, :, None] + update
            return (newest, total, accum)

        start_carry = (
            jnp.full((heads_here, block), -1e30, jnp.float32),
            jnp.zeros((heads_here, block), jnp.float32),
            jnp.zeros((heads_here, block, HEAD_DIM), jnp.float32),
        )
        running, total, accum = lax.fori_loop(lowest, which + 1, key_block, start_carry)
        result = (accum / total[:, :, None]).astype(jnp.bfloat16)
        return result.transpose(1, 0, 2)

    blocks_out = lax.map(query_block, jnp.arange(count, dtype=jnp.int32))
    return blocks_out.reshape(seq_len, heads_here, HEAD_DIM)


def body(queries, key_rows, value_rows, doc_blocks, phm_mix, phm_blocks):
    tok_rows = queries.shape[0]
    heads = queries.shape[1] // HEAD_DIM
    shaped = (
        queries.reshape(tok_rows, heads, HEAD_DIM),
        key_rows.reshape(tok_rows, heads, HEAD_DIM),
        value_rows.reshape(tok_rows, heads, HEAD_DIM),
    )
    q_all, k_all, v_all = (
        lax.all_to_all(shaped[0], "ctx", split_axis=1, concat_axis=0, tiled=True),
        lax.all_to_all(shaped[1], "ctx", split_axis=1, concat_axis=0, tiled=True),
        lax.all_to_all(shaped[2], "ctx", split_axis=1, concat_axis=0, tiled=True),
    )
    seq_len = q_all.shape[0]
    lengths = doc_blocks * UNIT
    ends = jnp.cumsum(lengths)
    positions = jnp.arange(seq_len, dtype=jnp.int32)
    doc_ids = jnp.sum((positions[:, None] >= ends[None, :]).astype(jnp.int32), axis=1)
    attended = attend(q_all, k_all, v_all, doc_ids)
    returned = lax.all_to_all(attended, "ctx", split_axis=0, concat_axis=1, tiled=True)
    rows_phm = heads * HEAD_DIM // PHM_N
    pieces = returned.reshape(tok_rows, PHM_N, rows_phm).astype(jnp.float32)
    mixed = jnp.einsum("iab,tar->tbir", phm_mix, pieces, precision=lax.Precision.HIGHEST)
    mixed = mixed.astype(jnp.bfloat16).reshape(tok_rows, PHM_N, PHM_N * rows_phm)
    cols_phm = phm_blocks.shape[1]
    output = jnp.einsum(
        "tbk,kc->tbc",
        mixed,
        lax.all_gather(phm_blocks, "ctx", axis=0, tiled=True),
        preferred_element_type=jnp.float32,
    )
    return output.reshape(tok_rows, PHM_N * cols_phm).astype(jnp.bfloat16)


def solution(mesh):
    placed = (
        P(("rep", "ctx"), None),
        P(("rep", "ctx"), None),
        P(("rep", "ctx"), None),
        P("rep"),
        P(),
        P("ctx", None),
    )
    return jax.shard_map(
        body, mesh=mesh, in_specs=placed, out_specs=P(("rep", "ctx"), None), check_vma=False
    )
```

profile of v0, /device:TPU:2, one launch (start us, length us, event | category | flops | bytes accessed | tf_op | source)
XLA Modules:
  0.0 334.3 jit_solution(11161322428477546401)
XLA Ops:
  6.5 2.4 copy.56
  9.0 11.5 %all-to-all-start.1 = ((bf16[128,32,128]{0,2,1:T(8,128)(2,1)}), bf16[128,32,128]{0,2,1:T(8,128)(2,1)S(1)}, u32[]{:S(2)}, u32[]{:S(2)}) async-start(bf16[128,32,128]{0,2,1:T(8,128)(2,1)} %bitcast.10), calls=%async_computation.1 | async-start | bytes 2097152 | tf_op jit(solution)/shard_map/all_to_all | solution.py:75
  20.5 1.3 copy.58
  21.8 27.3 %all-to-all-done.1 = bf16[128,32,128]{0,2,1:T(8,128)(2,1)S(1)} async-done(((bf16[128,32,128]{0,2,1:T(8,128)(2,1)}), bf16[128,32,128]{0,2,1:T(8,128)(2,1)S(1)}, u32[]{:S(2)}, u32[]{:S(2)}) %all-to-all-start.1) | async-done | bytes 1048608 | tf_op jit(solution)/shard_map/all_to_all | solution.py:75
  49.1 5.1 %all-to-all-start.2 = ((bf16[128,32,128]{0,2,1:T(8,128)(2,1)}), bf16[128,32,128]{0,2,1:T(8,128)(2,1)S(1)}, u32[]{:S(2)}, u32[]{:S(2)}) async-start(bf16[128,32,128]{0,2,1:T(8,128)(2,1)} %bitcast.14), calls=%async_computation.2 | async-start | bytes 2097152 | tf_op jit(solution)/shard_map/all_to_all | solution.py:76
  54.2 1.3 copy.54
  55.5 26.9 %all-to-all-done.2 = bf16[128,32,128]{0,2,1:T(8,128)(2,1)S(1)} async-done(((bf16[128,32,128]{0,2,1:T(8,128)(2,1)}), bf16[128,32,128]{0,2,1:T(8,128)(2,1)S(1)}, u32[]{:S(2)}, u32[]{:S(2)}) %all-to-all-start.2) | async-done | bytes 1048608 | tf_op jit(solution)/shard_map/all_to_all | solution.py:76
  82.4 4.9 %all-to-all-start = ((bf16[128,32,128]{0,2,1:T(8,128)(2,1)}), bf16[128,32,128]{0,2,1:T(8,128)(2,1)S(1)}, u32[]{:S(2)}, u32[]{:S(2)}) async-start(bf16[128,32,128]{0,2,1:T(8,128)(2,1)} %bitcast.6), calls=%async_computation | async-start | bytes 2097152 | tf_op jit(solution)/shard_map/all_to_all | solution.py:74
  88.4 1.3 copy.57
  89.8 1.3 copy.59
  91.1 25.6 %all-to-all-done = bf16[128,32,128]{0,2,1:T(8,128)(2,1)S(1)} async-done(((bf16[128,32,128]{0,2,1:T(8,128)(2,1)}), bf16[128,32,128]{0,2,1:T(8,128)(2,1)S(1)}, u32[]{:S(2)}, u32[]{:S(2)}) %all-to-all-start) | async-done | bytes 1048608 | tf_op jit(solution)/shard_map/all_to_all | solution.py:74
  117.4 142.4 %while.26 = (s32[]{:T(128)}, bf16[8,512,1,128]{3,1,2,0:T(8,128)(2,1)}, s32[8]{0:T(128)S(1)}, s32[4096]{0:T(1024)S(1)}, bf16[4096,1,128]{2,0,1:T(8,128)(2,1)S(1)}...) while((s32[]{:T(128)}, ...), condition=%wide.region_7.8_spmd, body=%wide.region_2.7_spmd.sunk | while | flops 139200512 | bytes 5057614 | solution.py:61
  119.5 3.3 while.27
  121.3 1.5 fusion.41
  125.8 6.6 %while.27 = (s32[]{:T(128)}, f32[1,512]{1,0:T(1,128)S(1)}, f32[1,512]{1,0:T(1,128)S(1)}, f32[1,512,128]{2,1,0:T(8,128)S(1)}, s32[]{:T(128)}, /*index=5*/s32[4096...) while((s32[]{:T(128)}, f32[1,512]{1,0:T(1,128)S(1)}, ...), condition=%wide.region_6.6_spmd.clone, body=%wide.region_3.5_spmd.clone.sunk | while | flops 139069440 | bytes 4128975 | solution.py:57
  127.6 1.5 fusion.41
  130.9 1.5 fusion.41
  135.4 9.9 %while.27 = (s32[]{:T(128)}, f32[1,512]{1,0:T(1,128)S(1)}, f32[1,512]{1,0:T(1,128)S(1)}, f32[1,512,128]{2,1,0:T(8,128)S(1)}, s32[]{:T(128)}, /*index=5*/s32[4096...) while((s32[]{:T(128)}, f32[1,512]{1,0:T(1,128)S(1)}, ...), condition=%wide.region_6.6_spmd.clone, body=%wide.region_3.5_spmd.clone.sunk | while | flops 139069440 | bytes 4128975 | solution.py:57
  137.1 1.5 fusion.41
  140.4 1.5 fusion.41
  143.7 1.5 fusion.41
  148.2 13.2 %while.27 = (s32[]{:T(128)}, f32[1,512]{1,0:T(1,128)S(1)}, f32[1,512]{1,0:T(1,128)S(1)}, f32[1,512,128]{2,1,0:T(8,128)S(1)}, s32[]{:T(128)}, /*index=5*/s32[4096...) while((s32[]{:T(128)}, f32[1,512]{1,0:T(1,128)S(1)}, ...), condition=%wide.region_6.6_spmd.clone, body=%wide.region_3.5_spmd.clone.sunk | while | flops 139069440 | bytes 4128975 | solution.py:57
  150.0 1.5 fusion.41
  153.3 1.5 fusion.41
  156.6 1.5 fusion.41
  159.9 1.5 fusion.41
  164.4 16.5 %while.27 = (s32[]{:T(128)}, f32[1,512]{1,0:T(1,128)S(1)}, f32[1,512]{1,0:T(1,128)S(1)}, f32[1,512,128]{2,1,0:T(8,128)S(1)}, s32[]{:T(128)}, /*index=5*/s32[4096...) while((s32[]{:T(128)}, f32[1,512]{1,0:T(1,128)S(1)}, ...), condition=%wide.region_6.6_spmd.clone, body=%wide.region_3.5_spmd.clone.sunk | while | flops 139069440 | bytes 4128975 | solution.py:57
  166.2 1.5 fusion.41
  169.5 1.5 fusion.41
  171.1 1.3 fusion.39
  172.8 1.5 fusion.41
  176.1 1.5 fusion.41
  177.7 1.3 fusion.39
  179.4 1.5 fusion.41
  183.9 19.8 %while.27 = (s32[]{:T(128)}, f32[1,512]{1,0:T(1,128)S(1)}, f32[1,512]{1,0:T(1,128)S(1)}, f32[1,512,128]{2,1,0:T(8,128)S(1)}, s32[]{:T(128)}, /*index=5*/s32[4096...) while((s32[]{:T(128)}, f32[1,512]{1,0:T(1,128)S(1)}, ...), condition=%wide.region_6.6_spmd.clone, body=%wide.region_3.5_spmd.clone.sunk | while | flops 139069440 | bytes 4128975 | solution.py:57
  185.7 1.5 fusion.41
  188.9 1.5 fusion.41
  192.2 1.5 fusion.41
  195.5 1.5 fusion.41
  198.8 1.5 fusion.41
  202.1 1.5 fusion.41
  206.6 23.0 %while.27 = (s32[]{:T(128)}, f32[1,512]{1,0:T(1,128)S(1)}, f32[1,512]{1,0:T(1,128)S(1)}, f32[1,512,128]{2,1,0:T(8,128)S(1)}, s32[]{:T(128)}, /*index=5*/s32[4096...) while((s32[]{:T(128)}, f32[1,512]{1,0:T(1,128)S(1)}, ...), condition=%wide.region_6.6_spmd.clone, body=%wide.region_3.5_spmd.clone.sunk | while | flops 139069440 | bytes 4128975 | solution.py:57
  208.4 1.5 fusion.41
  211.7 1.5 fusion.41
  215.0 1.5 fusion.41
  218.3 1.5 fusion.41
  221.5 1.5 fusion.41
  224.8 1.5 fusion.41
  228.1 1.5 fusion.41
  232.6 26.3 %while.27 = (s32[]{:T(128)}, f32[1,512]{1,0:T(1,128)S(1)}, f32[1,512]{1,0:T(1,128)S(1)}, f32[1,512,128]{2,1,0:T(8,128)S(1)}, s32[]{:T(128)}, /*index=5*/s32[4096...) while((s32[]{:T(128)}, f32[1,512]{1,0:T(1,128)S(1)}, ...), condition=%wide.region_6.6_spmd.clone, body=%wide.region_3.5_spmd.clone.sunk | while | flops 139069440 | bytes 4128975 | solution.py:57
  234.4 1.5 fusion.41
  237.7 1.5 fusion.41
  241.0 1.5 fusion.41
  244.3 1.5 fusion.41
  247.6 1.5 fusion.41
  250.8 1.5 fusion.41
  254.1 1.5 fusion.41
  257.4 1.5 fusion.41
  260.3 2.7 reduce.4
  263.3 33.1 %all_to_all.69 = bf16[32,2,8192]{2,1,0:T(2,128)(2,1)S(1)} all-to-all(bf16[32,2,8192]{2,1,0:T(2,128)(2,1)S(1)} %reshape.102), channel_id=1, replica_groups=mesh['ctx'=32,'rep'=8] {'ctx'}, dimensions={0} | all-to-all | bytes 2097152 | tf_op jit(solution)/shard_map/all_to_all | solution.py:84
  298.5 8.3 %fusion.24 = bf16[128,4,4,1024]{3,1,2,0:T(4,128)(2,1)} fusion(bf16[128,4,1024,1]{2,1,0,3:T(4,128)(2,1)S(1)} %reshape.98, f32[4,4,4]{2,1,0:T(4,128)S(1)} %copy-done), kind=kOutput, calls=%fused_computation.34 | convolution fusion | flops 102760448 | bytes 5243136 | tf_op jit(solution)/shard_map/iab,tar->tbir/dot_general | solution.py:87
  306.9 7.8 %copy.63 = bf16[128,4,4,1024]{0,3,2,1:T(8,128)(2,1)} copy(bf16[128,4,4,1024]{3,1,2,0:T(4,128)(2,1)} %fusion.24) | data formatting | bytes 8388608 | tf_op jit(solution)/shard_map/convert_element_type | solution.py:88
  314.7 10.5 %fusion.25 = bf16[128,4,1280]{2,0,1:T(8,128)(2,1)S(1)} fusion(bf16[128,4,4096]{0,2,1:T(8,128)(2,1)} %bitcast.101, bf16[4096,1280]{1,0:T(8,128)(2,1)} %all-gather.2.cloned.1.call-done), kind=kOutput, calls=%fused_computation.35 | convolution fusion | flops 5369364480 | bytes 15990784 | tf_op jit(solution)/shard_map/tbk,kc->tbc/dot_general | solution.py:90
  326.0 1.4 copy.66
  (330 shorter events, 77.1 us)
Async XLA Ops:
  6.5 292.0 %copy-start = (f32[4,4,4]{2,1,0:T(4,128)S(1)}, f32[4,4,4]{2,1,0:T(4,128)}, u32[]{:S(2)}) copy-start(f32[4,4,4]{2,1,0:T(4,128)} %param.14) | copy-start | bytes 772
  6.5 13.9 %copy-start.1 = (bf16[128,4096]{1,0:T(8,128)(2,1)S(1)}, bf16[128,4096]{1,0:T(8,128)(2,1)}, u32[]{:S(2)}) copy-start(bf16[128,4096]{1,0:T(8,128)(2,1)} %param.12) | copy-start | bytes 3145732
  6.5 47.6 %copy-start.2 = (bf16[128,4096]{1,0:T(8,128)(2,1)S(1)}, bf16[128,4096]{1,0:T(8,128)(2,1)}, u32[]{:S(2)}) copy-start(bf16[128,4096]{1,0:T(8,128)(2,1)} %param.10) | copy-start | bytes 3145732
  9.0 40.1 %all-to-all-start.1 = ((bf16[128,32,128]{0,2,1:T(8,128)(2,1)}), bf16[128,32,128]{0,2,1:T(8,128)(2,1)S(1)}, u32[]{:S(2)}, u32[]{:S(2)}) async-start(bf16[128,32,128]{0,2,1:T(8,128)(2,1)} %bitcast.10), calls=%async_computation.1 | async-start | bytes 2097152 | tf_op jit(solution)/shard_map/all_to_all | solution.py:75
  20.5 67.7 %copy-start.3 = (s32[3]{0:T(128)S(1)}, s32[3]{0:T(128)}, u32[]{:S(2)}) copy-start(s32[3]{0:T(128)} %param.13) | copy-start | bytes 40
  49.1 33.4 %all-to-all-start.2 = ((bf16[128,32,128]{0,2,1:T(8,128)(2,1)}), bf16[128,32,128]{0,2,1:T(8,128)(2,1)S(1)}, u32[]{:S(2)}, u32[]{:S(2)}) async-start(bf16[128,32,128]{0,2,1:T(8,128)(2,1)} %bitcast.14), calls=%async_computation.2 | async-start | bytes 2097152 | tf_op jit(solution)/shard_map/all_to_all | solution.py:76
  82.4 34.2 %all-to-all-start = ((bf16[128,32,128]{0,2,1:T(8,128)(2,1)}), bf16[128,32,128]{0,2,1:T(8,128)(2,1)S(1)}, u32[]{:S(2)}, u32[]{:S(2)}) async-start(bf16[128,32,128]{0,2,1:T(8,128)(2,1)} %bitcast.6), calls=%async_computation | async-start | bytes 2097152 | tf_op jit(solution)/shard_map/all_to_all | solution.py:74
  87.4 227.3 %all-gather.2.cloned.1.call-start = ((), (), s32[]{:S(2)}) async-start(), calls=%async_computation.4 | async-start | bytes 10813440 | tf_op jit(solution)/shard_map/all_gather | solution.py:93
Sparse Core Ops, SparseCore 0:
  90.8 111.4 all-gather.1
where the time goes:
time: 336 us; the launch traced here: 334 us
  matrix products  120 us (36%)
  waiting for transfers between devices  80.5 us (24%)
  blocking collectives  33.1 us (10%)
  local copies, waits for them, and re-layouts  30.4 us (9%)
  other arithmetic  21.7 us (6%)
  starting transfers between devices  21.6 us (6%)
  between operations  13.6 us (4%)
  loops' own time  13.3 us (4%)
    dot_general x36, matrix products, key_block(): jnp.einsum('hqk,khe->hqe', expd.astype(jnp.bfloat16), v_part, preferred_e...  54.9 us
    dot_general x36, matrix products, key_block(): jnp.einsum('qhe,khe->hqk', q_part, k_part, preferred_element_type=jnp.flo...  46.5 us
    all_to_all x1, blocking collectives, body(): lax.all_to_all(attended, 'ctx', split_axis=0, concat_axis=1, tiled=True)  33.1 us
    all_to_all x1, waiting for transfers between devices, body(): lax.all_to_all(shaped[1], 'ctx', split_axis=1, concat_axis=0, tiled=True)  27.3 us
    all_to_all x1, waiting for transfers between devices, body(): lax.all_to_all(shaped[2], 'ctx', split_axis=1, concat_axis=0, tiled=True)  26.9 us
    all_to_all x1, waiting for transfers between devices, body(): lax.all_to_all(shaped[0], 'ctx', split_axis=1, concat_axis=0, tiled=True)  25.6 us
    all_to_all x1, starting transfers between devices, body(): lax.all_to_all(shaped[1], 'ctx', split_axis=1, concat_axis=0, tiled=True)  11.5 us
    reduce_sum x36, other arithmetic, key_block(): total = total * factor + jnp.sum(expd, axis=2)  11.3 us
  transfers between devices with their start and end apart: 4, of which 3 were waited for; matrix products, arithmetic and copies ran while one was open for 47% of the time, Pallas kernels for 0%

commit v1 on v0

v1 whole, which is shorter than its diff:
```python
import functools
import math

import jax
import jax.numpy as jnp
from jax import lax
from jax.experimental import pallas as pl
from jax.experimental.pallas import tpu as pltpu
from jax.sharding import PartitionSpec as P

HEAD_DIM = 128
PHM_N = 4
UNIT = 128
BQ = 256
BK = 256


def flash_kernel(ends_ref, q_ref, k_ref, v_ref, o_ref):
    i = pl.program_id(0)
    e0 = ends_ref[0]
    e1 = ends_ref[1]
    scale = 1.0 / math.sqrt(HEAD_DIM)

    def doc_start(t):
        return jnp.where(t >= e1, e1, jnp.where(t >= e0, e0, 0))

    q_lo = i * BQ
    j_lo = doc_start(q_lo) // BK
    j_hi = (q_lo + BQ - 1) // BK
    q = q_ref[...]
    q_pos = q_lo + lax.broadcasted_iota(jnp.int32, (BQ, 1), 0)
    q_start = doc_start(q_pos)

    def body(j, carry):
        m, l, acc = carry
        base = pl.multiple_of(j * BK, BK)
        k = k_ref[pl.ds(base, BK), :]
        v = v_ref[pl.ds(base, BK), :]
        s = lax.dot_general(
            q, k, (((1,), (1,)), ((), ())), preferred_element_type=jnp.float32
        ) * scale
        k_pos = base + lax.broadcasted_iota(jnp.int32, (1, BK), 1)
        mask = (k_pos <= q_pos) & (k_pos >= q_start)
        s = jnp.where(mask, s, -1e30)
        m_new = jnp.maximum(m, jnp.max(s, axis=1, keepdims=True))
        p = jnp.where(mask, jnp.exp(s - m_new), 0.0)
        alpha = jnp.exp(m - m_new)
        l = alpha * l + jnp.sum(p, axis=1, keepdims=True)
        acc = alpha * acc + jnp.dot(
            p.astype(jnp.bfloat16), v, preferred_element_type=jnp.float32
        )
        return m_new, l, acc

    carry = (
        jnp.full((BQ, 1), -1e30, jnp.float32),
        jnp.zeros((BQ, 1), jnp.float32),
        jnp.zeros((BQ, HEAD_DIM), jnp.float32),
    )
    m, l, acc = lax.fori_loop(j_lo, j_hi + 1, body, carry)
    o_ref[...] = (acc / l).astype(o_ref.dtype)


def attend(q, k, v, ends):
    seq = q.shape[0]
    full = pl.BlockSpec((seq, HEAD_DIM), lambda i, e: (0, 0))
    return pl.pallas_call(
        flash_kernel,
        grid_spec=pltpu.PrefetchScalarGridSpec(
            num_scalar_prefetch=1,
            grid=(seq // BQ,),
            in_specs=[
                pl.BlockSpec((BQ, HEAD_DIM), lambda i, e: (i, 0)),
                full,
                full,
            ],
            out_specs=pl.BlockSpec((BQ, HEAD_DIM), lambda i, e: (i, 0)),
        ),
        out_shape=jax.ShapeDtypeStruct((seq, HEAD_DIM), jnp.bfloat16),
    )(ends, q, k, v)


def body(queries, key_rows, value_rows, doc_blocks, phm_mix, phm_blocks):
    tok_rows = queries.shape[0]
    heads = queries.shape[1] // HEAD_DIM
    stacked = jnp.stack([queries, key_rows, value_rows]).reshape(3, tok_rows, heads, HEAD_DIM)
    gathered = lax.all_to_all(stacked, "ctx", split_axis=2, concat_axis=1, tiled=True)
    seq_len = gathered.shape[1]
    q_all = gathered[0].reshape(seq_len, HEAD_DIM)
    k_all = gathered[1].reshape(seq_len, HEAD_DIM)
    v_all = gathered[2].reshape(seq_len, HEAD_DIM)
    ends = jnp.cumsum(doc_blocks.astype(jnp.int32) * UNIT).astype(jnp.int32)
    attended = attend(q_all, k_all, v_all, ends).reshape(seq_len, 1, HEAD_DIM)
    returned = lax.all_to_all(attended, "ctx", split_axis=0, concat_axis=1, tiled=True)
    rows_phm = heads * HEAD_DIM // PHM_N
    pieces = returned.reshape(tok_rows, PHM_N, rows_phm).astype(jnp.float32)
    mixed = jnp.einsum("iab,tar->tbir", phm_mix, pieces, precision=lax.Precision.HIGHEST)
    mixed = mixed.astype(jnp.bfloat16).reshape(tok_rows, PHM_N, PHM_N * rows_phm)
    cols_phm = phm_blocks.shape[1]
    output = jnp.einsum(
        "tbk,kc->tbc",
        mixed,
        lax.all_gather(phm_blocks, "ctx", axis=0, tiled=True),
        preferred_element_type=jnp.float32,
    )
    return output.reshape(tok_rows, PHM_N * cols_phm).astype(jnp.bfloat16)


def solution(mesh):
    placed = (
        P(("rep", "ctx"), None),
        P(("rep", "ctx"), None),
        P(("rep", "ctx"), None),
        P("rep"),
        P(),
        P("ctx", None),
    )
    return jax.shard_map(
        body, mesh=mesh, in_specs=placed, out_specs=P(("rep", "ctx"), None), check_vma=False
    )
```

time: 336 us -> 235 us (0.70)
  matrix products: 120 us -> 18.8 us
  Pallas kernels: 0 us -> 36.9 us
  other arithmetic: 21.7 us -> 5.61 us
  loops' own time: 13.3 us -> 0 us
  waiting for transfers between devices: 80.5 us -> 91.5 us
  starting transfers between devices: 21.6 us -> 11.6 us
  local copies, waits for them, and re-layouts: 30.4 us -> 22.5 us
    dot_general x72 -> x0, matrix products: 101 us -> none  [the longest x36 54.9 us: key_block(): jnp.einsum('hqk,khe->hqe', expd.astype(jnp.bfloat16), v_part, preferred_e...]
    pallas_call x0 -> x1, Pallas kernels: none -> 36.9 us  [attend(): pl.pallas_call(flash_kernel, grid_spec=pltpu.PrefetchScalarGridSpec(num_s...]
    another operation x9 -> x0, loops' own time: 13.3 us -> none  [the longest x1 11.3 us: attend(): blocks_out = lax.map(query_block, jnp.arange(count, dtype=jnp.int32))]
    reduce_sum x37 -> x0, other arithmetic: 11.5 us -> none  [the longest x36 11.3 us: key_block(): total = total * factor + jnp.sum(expd, axis=2)]
    all_to_all x3 -> x1, waiting for transfers between devices: 79.8 us -> 90.8 us  [body(): lax.all_to_all(stacked, 'ctx', split_axis=2, concat_axis=1, tiled=True)]
    all_to_all x3 -> x1, starting transfers between devices: 21.5 us -> 11.6 us  [body(): lax.all_to_all(stacked, 'ctx', split_axis=2, concat_axis=1, tiled=True)]
    dynamic_slice x60 -> x0, local copies, waits for them, and re-layouts: 8.71 us -> none  [the longest x8 5.21 us: attend(): blocks_out = lax.map(query_block, jnp.arange(count, dtype=jnp.int32))]
    dynamic_update_slice x8 -> x0, other arithmetic: 6.43 us -> none  [attend(): blocks_out = lax.map(query_block, jnp.arange(count, dtype=jnp.int32))]
  transfers between devices with their start and end apart: 4 -> 2, of which waited for: 3 -> 1; matrix products, arithmetic and copies ran while one was open for 47% -> 14% of each run, Pallas kernels for 0% -> 16%
where the time goes in v1:
time: 235 us; the launch traced here: 236 us
  waiting for transfers between devices  91.5 us (39%)
  Pallas kernels  36.9 us (16%)
  blocking collectives  35.7 us (15%)
  local copies, waits for them, and re-layouts  22.5 us (10%)
  matrix products  18.8 us (8%)
  between operations  13.5 us (6%)
  starting transfers between devices  11.6 us (5%)
  other arithmetic  5.61 us (2%)
    all_to_all x1, waiting for transfers between devices, body(): lax.all_to_all(stacked, 'ctx', split_axis=2, concat_axis=1, tiled=True)  90.8 us
    pallas_call x1, Pallas kernels, attend(): pl.pallas_call(flash_kernel, grid_spec=pltpu.PrefetchScalarGridSpec(num_s...  36.9 us
    all_to_all x1, blocking collectives, body(): lax.all_to_all(attended, 'ctx', split_axis=0, concat_axis=1, tiled=True)  35.7 us
    all_to_all x1, starting transfers between devices, body(): lax.all_to_all(stacked, 'ctx', split_axis=2, concat_axis=1, tiled=True)  11.6 us
    dot_general x1, matrix products, body(): jnp.einsum('tbk,kc->tbc', mixed, lax.all_gather(phm_blocks, 'ctx', axis=0...  10.5 us
    dot_general x1, matrix products, body(): jnp.einsum('iab,tar->tbir', phm_mix, pieces, precision=lax.Precision.HIGH...  8.36 us
    convert_element_type x1, local copies, waits for them, and re-layouts, body(): mixed.astype(jnp.bfloat16).reshape(tok_rows, PHM_N, PHM_N * rows_phm)  7.85 us
    unnamed x14, local copies, waits for them, and re-layouts  6.34 us
  transfers between devices with their start and end apart: 2, of which 1 were waited for; matrix products, arithmetic and copies ran while one was open for 14% of the time, Pallas kernels for 16%

profile of v1, /device:TPU:2, one launch (start us, length us, event | category | flops | bytes accessed | tf_op | source)
XLA Modules:
  0.0 236.2 jit_solution(1819294932760921510)
XLA Ops:
  6.5 0.0 copy-start
  6.5 0.0 copy-start.1
  6.5 0.0 copy-start.2
  6.5 0.0 all-gather.2.cloned.1.call-start
  6.5 0.7 all-gather.2.cloned.1.call-update
  7.3 2.3 copy.28
  9.5 0.0 copy-done.1
  9.5 1.3 copy.29
  10.8 0.0 copy-done.2
  10.8 1.3 copy.30
  12.1 2.2 pad_maximum_fusion
  14.3 2.8 %copy.31 = bf16[3,128,32,128]{3,1,0,2:T(8,128)(2,1)} copy(bf16[3,128,32,128]{1,3,2,0:T(8,128)(2,1)S(1)} %pad_maximum_fusion) | data formatting | bytes 6291456 | tf_op jit(solution)/shard_map/stack | solution.py:85
  17.2 0.0 copy-start.3
  17.2 11.6 %all-to-all-start = ((bf16[3,128,32,128]{3,1,0,2:T(8,128)(2,1)}), bf16[3,128,32,128]{3,1,0,2:T(8,128)(2,1)S(1)}, u32[]{:S(2)}, u32[]{:S(2)}) async-start(bf16[3,128,32,128]{3,1,0,2:T(8,128)(2,1)} %copy.31), calls=%async_computation | async-start | bytes 6291456 | tf_op jit(solution)/shard_map/all_to_all | solution.py:86
  28.8 0.0 copy-done.3
  28.8 0.7 reduce-window.9
  29.6 90.8 %all-to-all-done = bf16[3,128,32,128]{3,1,0,2:T(8,128)(2,1)S(1)} async-done(((bf16[3,128,32,128]{3,1,0,2:T(8,128)(2,1)}), bf16[3,128,32,128]{3,1,0,2:T(8,128)(2,1)S(1)}, u32[]{:S(2)}, u32[]{:S(2)}) %all-to-all-start) | async-done | bytes 3145760 | tf_op jit(solution)/shard_map/all_to_all | solution.py:86
  120.4 1.7 fusion.8
  122.2 36.9 %shard_map.64 = bf16[4096,128]{1,0:T(8,128)(2,1)} custom-call(s32[3]{0:T(128)} %bitcast.47, bf16[4096,128]{1,0:T(8,128)(2,1)} %bitcast.43, bf16[4096,128]{1,0:T(8,128)(2,1)} %bitcast.42, bf16[4096,128]{1,0:T(8,128)(2,1)} %bitcast.41), custom_call_target="tpu_custom_call" | custom-call | tf_op jit(solution)/shard_map/pallas_call | solution.py:66
  159.0 0.5 broadcast.5
  159.6 2.7 %reduce = bf16[4096,128]{1,0:T(8,128)(2,1)S(1)} reduce(bf16[4096,1,128]{2,0,1:T(8,128)(2,1)} %bitcast.38, bf16[]{:T(256)} %broadcast.5), dimensions={1}, to_apply=%copy.32.reduce_sub_computation | reduce | bytes 2097154 | tf_op jit(solution)/shard_map/reshape | solution.py:92
  162.2 0.3 reshape.60
  162.5 35.7 %all_to_all.30 = bf16[32,2,8192]{2,1,0:T(2,128)(2,1)S(1)} all-to-all(bf16[32,2,8192]{2,1,0:T(2,128)(2,1)S(1)} %reshape.60), channel_id=1, replica_groups=mesh['ctx'=32,'rep'=8] {'ctx'}, dimensions={0} | all-to-all | bytes 2097152 | tf_op jit(solution)/shard_map/all_to_all | solution.py:93
  198.2 1.0 reshape.61
  199.2 0.1 copy.43
  199.4 0.7 copy.33
  200.1 0.3 reshape.56
  200.4 0.0 copy-done
  200.4 8.4 %fusion.2 = bf16[128,4,4,1024]{3,1,2,0:T(4,128)(2,1)} fusion(bf16[128,4,1024,1]{2,1,0,3:T(4,128)(2,1)S(1)} %reshape.56, f32[4,4,4]{2,1,0:T(4,128)S(1)} %copy-done), kind=kOutput, calls=%fused_computation.3 | convolution fusion | flops 102760448 | bytes 5243136 | tf_op jit(solution)/shard_map/iab,tar->tbir/dot_general | solution.py:96
  208.8 7.9 %copy.35 = bf16[128,4,4,1024]{0,3,2,1:T(8,128)(2,1)} copy(bf16[128,4,4,1024]{3,1,2,0:T(4,128)(2,1)} %fusion.2) | data formatting | bytes 8388608 | tf_op jit(solution)/shard_map/convert_element_type | solution.py:97
  216.6 0.0 all-gather.2.cloned.1.call-done
  216.6 10.5 %fusion.3 = bf16[128,4,1280]{2,0,1:T(8,128)(2,1)S(1)} fusion(bf16[128,4,4096]{0,2,1:T(8,128)(2,1)} %bitcast.40, bf16[4096,1280]{1,0:T(8,128)(2,1)} %all-gather.2.cloned.1.call-done), kind=kOutput, calls=%fused_computation.5 | convolution fusion | flops 5369364480 | bytes 15990784 | tf_op jit(solution)/shard_map/tbk,kc->tbc/dot_general | solution.py:99
  227.1 0.8 copy.37
  227.9 1.4 copy.38
  (1 shorter events, 0.0 us)
Async XLA Ops:
  6.5 193.8 %copy-start = (f32[4,4,4]{2,1,0:T(4,128)S(1)}, f32[4,4,4]{2,1,0:T(4,128)}, u32[]{:S(2)}) copy-start(f32[4,4,4]{2,1,0:T(4,128)} %param.10) | copy-start | bytes 772
  6.5 3.0 %copy-start.1 = (bf16[128,4096]{1,0:T(8,128)(2,1)S(1)}, bf16[128,4096]{1,0:T(8,128)(2,1)}, u32[]{:S(2)}) copy-start(bf16[128,4096]{1,0:T(8,128)(2,1)} %param.7) | copy-start | bytes 3145732
  6.5 4.3 %copy-start.2 = (bf16[128,4096]{1,0:T(8,128)(2,1)S(1)}, bf16[128,4096]{1,0:T(8,128)(2,1)}, u32[]{:S(2)}) copy-start(bf16[128,4096]{1,0:T(8,128)(2,1)} %param.8) | copy-start | bytes 3145732
  6.5 210.1 %all-gather.2.cloned.1.call-start = ((), (), s32[]{:S(2)}) async-start(), calls=%async_computation.2 | async-start | bytes 10813440 | tf_op jit(solution)/shard_map/all_gather | solution.py:102
  17.2 11.6 %copy-start.3 = (s32[3]{0:T(128)S(1)}, s32[3]{0:T(128)}, u32[]{:S(2)}) copy-start(s32[3]{0:T(128)} %param.9) | copy-start | bytes 40
  17.2 103.2 %all-to-all-start = ((bf16[3,128,32,128]{3,1,0,2:T(8,128)(2,1)}), bf16[3,128,32,128]{3,1,0,2:T(8,128)(2,1)S(1)}, u32[]{:S(2)}, u32[]{:S(2)}) async-start(bf16[3,128,32,128]{3,1,0,2:T(8,128)(2,1)} %copy.31), calls=%async_computation | async-start | bytes 6291456 | tf_op jit(solution)/shard_map/all_to_all | solution.py:86
Sparse Core Ops, SparseCore 0:
  9.9 149.9 all-gather.1

commit v2 on v1

--- a/solution.py
+++ b/solution.py
@@ -79,9 +79,64 @@
     )(ends, q, k, v)
 
 
+def proj_kernel(mix_ref, att_ref, w_ref, o_ref, acc_ref):
+    i = pl.program_id(0)
+    rows = w_ref.shape[0]
+    cols = w_ref.shape[1]
+
+    @pl.when(i == 0)
+    def _():
+        acc_ref[...] = jnp.zeros_like(acc_ref)
+
+    pieces = [att_ref[:, a * rows:(a + 1) * rows].astype(jnp.float32) for a in range(PHM_N)]
+    w = w_ref[...]
+    for b in range(PHM_N):
+        mixed = pieces[0] * mix_ref[(i * PHM_N + 0) * PHM_N + b]
+        for a in range(1, PHM_N):
+            mixed = mixed + pieces[a] * mix_ref[(i * PHM_N + a) * PHM_N + b]
+        acc_ref[b] += jnp.dot(mixed.astype(jnp.bfloat16), w, preferred_element_type=jnp.float32)
+
+    @pl.when(i == PHM_N - 1)
+    def _():
+        for b in range(PHM_N):
+            o_ref[:, b * cols:(b + 1) * cols] = acc_ref[b].astype(o_ref.dtype)
+
+
+def project(att, mix, w):
+    tok, width = att.shape
+    rows = width // PHM_N
+    cols = w.shape[1]
+    return pl.pallas_call(
+        proj_kernel,
+        grid=(PHM_N,),
+        in_specs=[
+            pl.BlockSpec(memory_space=pltpu.SMEM),
+            pl.BlockSpec((tok, width), lambda i: (0, 0)),
+            pl.BlockSpec((rows, cols), lambda i: (i, 0)),
+        ],
+        out_specs=pl.BlockSpec((tok, PHM_N * cols), lambda i: (0, 0)),
+        out_shape=jax.ShapeDtypeStruct((tok, PHM_N * cols), jnp.bfloat16),
+        scratch_shapes=[pltpu.VMEM((PHM_N, tok, cols), jnp.float32)],
+    )(mix.reshape(-1), att, w)
+
+
+def gather_factors(phm_blocks):
+    shard, cols = phm_blocks.shape
+    n_x = lax.axis_size("x")
+    n_core = lax.axis_size("core")
+    piece = shard // (n_x * n_core)
+    rho = lax.axis_index("x") * n_core + lax.axis_index("core")
+    mine = lax.dynamic_slice_in_dim(phm_blocks, rho * piece, piece, 0)
+    over_ctx = lax.all_gather(mine, "ctx", axis=0)
+    over_x = lax.all_gather(over_ctx, "x", axis=0)
+    over_core = lax.all_gather(over_x, "core", axis=0)
+    return over_core.transpose(2, 1, 0, 3, 4).reshape(-1, cols)
+
+
 def body(queries, key_rows, value_rows, doc_blocks, phm_mix, phm_blocks):
     tok_rows = queries.shape[0]
     heads = queries.shape[1] // HEAD_DIM
+    factors = gather_factors(phm_blocks)
     stacked = jnp.stack([queries, key_rows, value_rows]).reshape(3, tok_rows, heads, HEAD_DIM)
     gathered = lax.all_to_all(stacked, "ctx", split_axis=2, concat_axis=1, tiled=True)
     seq_len = gathered.shape[1]
@@ -91,29 +146,16 @@
     ends = jnp.cumsum(doc_blocks.astype(jnp.int32) * UNIT).astype(jnp.int32)
     attended = attend(q_all, k_all, v_all, ends).reshape(seq_len, 1, HEAD_DIM)
     returned = lax.all_to_all(attended, "ctx", split_axis=0, concat_axis=1, tiled=True)
-    rows_phm = heads * HEAD_DIM // PHM_N
-    pieces = returned.reshape(tok_rows, PHM_N, rows_phm).astype(jnp.float32)
-    mixed = jnp.einsum("iab,tar->tbir", phm_mix, pieces, precision=lax.Precision.HIGHEST)
-    mixed = mixed.astype(jnp.bfloat16).reshape(tok_rows, PHM_N, PHM_N * rows_phm)
-    cols_phm = phm_blocks.shape[1]
-    output = jnp.einsum(
-        "tbk,kc->tbc",
-        mixed,
-        lax.all_gather(phm_blocks, "ctx", axis=0, tiled=True),
-        preferred_element_type=jnp.float32,
-    )
-    return output.reshape(tok_rows, PHM_N * cols_phm).astype(jnp.bfloat16)
+    return project(returned.reshape(tok_rows, heads * HEAD_DIM), phm_mix, factors)
 
 
 def solution(mesh):
-    placed = (
-        P(("rep", "ctx"), None),
-        P(("rep", "ctx"), None),
-        P(("rep", "ctx"), None),
-        P("rep"),
-        P(),
-        P("ctx", None),
-    )
-    return jax.shard_map(
-        body, mesh=mesh, in_specs=placed, out_specs=P(("rep", "ctx"), None), check_vma=False
-    )
+    rep_at = mesh.axis_names.index("rep")
+    shape = list(mesh.devices.shape)
+    shape[rep_at:rep_at + 1] = [shape[rep_at] // 2, 2]
+    names = list(mesh.axis_names)
+    names[rep_at:rep_at + 1] = ["x", "core"]
+    split = jax.sharding.Mesh(mesh.devices.reshape(shape), tuple(names))
+    rows = P(("x", "core", "ctx"), None)
+    placed = (rows, rows, rows, P(("x", "core")), P(), P("ctx", None))
+    return jax.shard_map(body, mesh=split, in_specs=placed, out_specs=rows, check_vma=False)

time: 235 us -> 344 us (1.46); the launches traced: 236 us -> 342 us
  waiting for transfers between devices: 91.5 us -> 241 us
  blocking collectives: 35.7 us -> 0 us
  matrix products: 18.8 us -> 0 us
  starting transfers between devices: 11.6 us -> 15.9 us
  Pallas kernels: 36.9 us -> 40.6 us
    all_gather x1 -> x3, waiting for transfers between devices: 0.01 us -> 140 us  [the longest x1 81.3 us: gather_factors(): over_ctx = lax.all_gather(mine, 'ctx', axis=0)]
    all_to_all x1 -> x0, blocking collectives: 35.7 us -> none  [body(): lax.all_to_all(attended, 'ctx', split_axis=0, concat_axis=1, tiled=True)]
    all_to_all x0 -> x1, waiting for transfers between devices: none -> 27.8 us  [body(): lax.all_to_all(attended, 'ctx', split_axis=0, concat_axis=1, tiled=True)]
    dot_general x2 -> x0, matrix products: 18.8 us -> none  [the longest x1 10.5 us: body(): jnp.einsum('tbk,kc->tbc', mixed, lax.all_gather(phm_blocks, 'ctx', axis=0...]
    all_to_all x1, waiting for transfers between devices: 90.8 us -> 73.8 us  [body(): lax.all_to_all(stacked, 'ctx', split_axis=2, concat_axis=1, tiled=True)]
    pallas_call x0 -> x1, Pallas kernels: none -> 10.1 us  [project(): pl.pallas_call(proj_kernel, grid=(PHM_N,), in_specs=[pl.BlockSpec(memory_...]
    convert_element_type x3 -> x0, local copies, waits for them, and re-layouts: 10.1 us -> none  [the longest x1 7.85 us: body(): mixed.astype(jnp.bfloat16).reshape(tok_rows, PHM_N, PHM_N * rows_phm)]
    transpose x0 -> x1, local copies, waits for them, and re-layouts: none -> 9.43 us  [gather_factors(): return over_core.transpose(2, 1, 0, 3, 4).reshape(-1, cols)]
  transfers between devices with their start and end apart: 2 -> 5, of which waited for: 1 -> 4; matrix products, arithmetic and copies ran while one was open for 14% -> 6% of each run, Pallas kernels for 16% -> 9%
where the time goes in v2:
time: 344 us; the launch traced here: 342 us
  waiting for transfers between devices  241 us (70%)
  Pallas kernels  40.6 us (12%)
  local copies, waits for them, and re-layouts  25.1 us (7%)
  starting transfers between devices  15.9 us (5%)
  between operations  13.2 us (4%)
  other arithmetic  5.57 us (2%)
    all_gather x1, waiting for transfers between devices, gather_factors(): over_ctx = lax.all_gather(mine, 'ctx', axis=0)  81.3 us
    all_to_all x1, waiting for transfers between devices, body(): lax.all_to_all(stacked, 'ctx', split_axis=2, concat_axis=1, tiled=True)  73.8 us
    all_gather x1, waiting for transfers between devices, gather_factors(): over_x = lax.all_gather(over_ctx, 'x', axis=0)  58.3 us
    pallas_call x1, Pallas kernels, attend(): pl.pallas_call(flash_kernel, grid_spec=pltpu.PrefetchScalarGridSpec(num_s...  30.5 us
    all_to_all x1, waiting for transfers between devices, body(): lax.all_to_all(attended, 'ctx', split_axis=0, concat_axis=1, tiled=True)  27.8 us
    pallas_call x1, Pallas kernels, project(): pl.pallas_call(proj_kernel, grid=(PHM_N,), in_specs=[pl.BlockSpec(memory_...  10.1 us
    all_to_all x1, starting transfers between devices, body(): lax.all_to_all(stacked, 'ctx', split_axis=2, concat_axis=1, tiled=True)  9.98 us
    transpose x1, local copies, waits for them, and re-layouts, gather_factors(): return over_core.transpose(2, 1, 0, 3, 4).reshape(-1, cols)  9.43 us
  transfers between devices with their start and end apart: 5, of which 4 were waited for; matrix products, arithmetic and copies ran while one was open for 6% of the time, Pallas kernels for 9%

profile of v2, /device:TPU:2, one launch (start us, length us, event | category | flops | bytes accessed | tf_op | source)
XLA Modules:
  0.0 341.6 jit_solution(12778907686428663540)
XLA Ops:
  6.5 0.0 copy-start
  6.5 0.0 all-gather.7.cloned.1.call-start
  6.5 1.0 copy-done
  7.5 0.6 constant_dynamic-slice_fusion
  8.1 0.0 all-gather.7.cloned.1.call-update
  8.2 0.0 all-gather.9.cloned.1.call-start
  8.2 81.3 %all-gather.7.cloned.1.call-done = bf16[512,1280]{1,0:T(8,128)(2,1)} async-done(((bf16[16,1280]{1,0:T(8,128)(2,1)}), bf16[512,1280]{1,0:T(8,128)(2,1)}) %all-gather.7.cloned.1.call-update) | async-done | bytes 1310736 | tf_op jit(solution)/shard_map/all_gather | solution.py:130
  89.5 0.0 copy-start.1
  89.5 0.0 all-gather.9.cloned.1.call-update
  89.6 0.0 all-gather.11.cloned.1.call-start
  89.6 58.3 %all-gather.9.cloned.1.call-done = bf16[128,16,1280]{2,1,0:T(8,128)(2,1)} async-done(((bf16[32,16,1280]{2,1,0:T(8,128)(2,1)}), bf16[128,16,1280]{2,1,0:T(8,128)(2,1)}) %all-gather.9.cloned.1.call-update) | async-done | bytes 5242896 | tf_op jit(solution)/shard_map/all_gather | solution.py:131
  147.9 0.0 copy-start.2
  147.9 0.0 all-gather.11.cloned.1.call-update
  147.9 0.0 copy-done.1
  147.9 0.0 copy-start.3
  148.0 1.3 copy.19
  149.3 0.0 copy-done.2
  149.3 1.3 copy.20
  150.6 0.0 copy-done.3
  150.6 1.3 copy.21
  151.9 2.2 pad_maximum_fusion
  154.1 2.8 copy.22
  156.9 0.0 copy-start.5
  156.9 10.0 %all-to-all-start = ((bf16[3,128,32,128]{3,1,0,2:T(8,128)(2,1)}), bf16[3,128,32,128]{3,1,0,2:T(8,128)(2,1)S(1)}, u32[]{:S(2)}, u32[]{:S(2)}) async-start(bf16[3,128,32,128]{3,1,0,2:T(8,128)(2,1)} %copy.22), calls=%async_computation | async-start | bytes 6291456 | tf_op jit(solution)/shard_map/all_to_all | solution.py:141
  166.9 0.0 copy-done.5
  166.9 0.7 reduce-window.9
  167.6 73.8 %all-to-all-done = bf16[3,128,32,128]{3,1,0,2:T(8,128)(2,1)S(1)} async-done(((bf16[3,128,32,128]{3,1,0,2:T(8,128)(2,1)}), bf16[3,128,32,128]{3,1,0,2:T(8,128)(2,1)S(1)}, u32[]{:S(2)}, u32[]{:S(2)}) %all-to-all-start) | async-done | bytes 3145760 | tf_op jit(solution)/shard_map/all_to_all | solution.py:141
  241.4 1.7 fusion
  243.1 30.5 %shard_map.64 = bf16[4096,128]{1,0:T(8,128)(2,1)} custom-call(s32[3]{0:T(128)} %bitcast.43, bf16[4096,128]{1,0:T(8,128)(2,1)} %bitcast.37, bf16[4096,128]{1,0:T(8,128)(2,1)} %bitcast.36, bf16[4096,128]{1,0:T(8,128)(2,1)} %bitcast.35), custom_call_target="tpu_custom_call" | custom-call | tf_op jit(solution)/shard_map/pallas_call | solution.py:66
  273.6 0.5 broadcast.5
  274.2 0.0 copy-start.4
  274.2 2.7 reduce
  276.8 1.1 reshape.61
  277.9 5.8 %all-to-all-start.1 = ((bf16[32,2,8192]{2,1,0:T(2,128)(2,1)}), bf16[32,2,8192]{2,1,0:T(2,128)(2,1)S(1)}, u32[]{:S(2)}, u32[]{:S(2)}) async-start(bf16[32,2,8192]{2,1,0:T(2,128)(2,1)} %reshape.61), calls=%async_computation.1 | async-start | bytes 2097152 | tf_op jit(solution)/shard_map/all_to_all | solution.py:148
  283.7 0.0 copy-done.4
  283.8 0.7 reshape.52.mix_ref
  284.4 27.8 %all-to-all-done.1 = bf16[32,2,8192]{2,1,0:T(2,128)(2,1)S(1)} async-done(((bf16[32,2,8192]{2,1,0:T(2,128)(2,1)}), bf16[32,2,8192]{2,1,0:T(2,128)(2,1)S(1)}, u32[]{:S(2)}, u32[]{:S(2)}) %all-to-all-start.1) | async-done | bytes 1048608 | tf_op jit(solution)/shard_map/all_to_all | solution.py:148
  312.3 1.0 reshape.62
  313.3 0.1 copy.26
  313.4 0.7 copy.24
  314.1 1.4 copy.29
  315.6 0.0 all-gather.11.cloned.1.call-done
  315.6 9.4 %copy.25 = bf16[32,4,2,16,1280]{4,3,2,1,0:T(8,128)(2,1)} copy(bf16[32,4,2,16,1280]{4,3,0,1,2:T(8,128)(2,1)} %bitcast.30) | data formatting | bytes 20971520 | tf_op jit(solution)/shard_map/transpose | solution.py:133
  325.0 10.1 %shard_map.65 = bf16[128,5120]{1,0:T(8,128)(2,1)} custom-call(f32[64]{0:T(128)} %reshape.52.mix_ref, bf16[128,4096]{1,0:T(8,128)(2,1)} %bitcast.33, bf16[4096,1280]{1,0:T(8,128)(2,1)} %bitcast.28), custom_call_target="tpu_custom_call" | custom-call | tf_op jit(solution)/shard_map/pallas_call | solution.py:109
  (1 shorter events, 0.0 us)
Async XLA Ops:
  6.5 1.0 copy-start
  6.5 83.0 %all-gather.7.cloned.1.call-start = ((), (), s32[]{:S(2)}) async-start(), calls=%async_computation.2 | async-start | bytes 1351680 | tf_op jit(solution)/shard_map/all_gather | solution.py:130
  8.2 139.7 %all-gather.9.cloned.1.call-start = ((), (), s32[]{:S(2)}) async-start(), calls=%async_computation.3 | async-start | bytes 6553600 | tf_op jit(solution)/shard_map/all_gather | solution.py:131
  89.5 58.4 %copy-start.1 = (bf16[128,4096]{1,0:T(8,128)(2,1)S(1)}, bf16[128,4096]{1,0:T(8,128)(2,1)}, u32[]{:S(2)}) copy-start(bf16[128,4096]{1,0:T(8,128)(2,1)} %param.6) | copy-start | bytes 3145732
  89.6 226.0 %all-gather.11.cloned.1.call-start = ((), (), s32[]{:S(2)}) async-start(), calls=%async_computation.4 | async-start | bytes 15728640 | tf_op jit(solution)/shard_map/all_gather | solution.py:132
  147.9 1.4 copy-start.2
  147.9 2.6 copy-start.3
  156.9 10.0 %copy-start.5 = (s32[3]{0:T(128)S(1)}, s32[3]{0:T(128)}, u32[]{:S(2)}) copy-start(s32[3]{0:T(128)} %param.9) | copy-start | bytes 40
  156.9 84.5 %all-to-all-start = ((bf16[3,128,32,128]{3,1,0,2:T(8,128)(2,1)}), bf16[3,128,32,128]{3,1,0,2:T(8,128)(2,1)S(1)}, u32[]{:S(2)}, u32[]{:S(2)}) async-start(bf16[3,128,32,128]{3,1,0,2:T(8,128)(2,1)} %copy.22), calls=%async_computation | async-start | bytes 6291456 | tf_op jit(solution)/shard_map/all_to_all | solution.py:141
  274.2 9.6 %copy-start.4 = (f32[4,4,4]{2,1,0:T(4,128)S(1)}, f32[4,4,4]{2,1,0:T(4,128)}, u32[]{:S(2)}) copy-start(f32[4,4,4]{2,1,0:T(4,128)} %param.10) | copy-start | bytes 772
  277.9 34.3 %all-to-all-start.1 = ((bf16[32,2,8192]{2,1,0:T(2,128)(2,1)}), bf16[32,2,8192]{2,1,0:T(2,128)(2,1)S(1)}, u32[]{:S(2)}, u32[]{:S(2)}) async-start(bf16[32,2,8192]{2,1,0:T(2,128)(2,1)} %reshape.61), calls=%async_computation.1 | async-start | bytes 2097152 | tf_op jit(solution)/shard_map/all_to_all | solution.py:148
Sparse Core Ops, SparseCore 0:
  9.9 79.5 all-gather.6
  91.3 56.5 all-gather.8
  149.7 28.9 all-gather.10

commit v3 on v2

v3 whole, which is shorter than its diff:
```python
import functools
import math

import jax
import jax.numpy as jnp
from jax import lax
from jax.experimental import pallas as pl
from jax.experimental.pallas import tpu as pltpu
from jax.sharding import PartitionSpec as P

HEAD_DIM = 128
PHM_N = 4
UNIT = 128
BQ = 256
BK = 256


def flash_kernel(ends_ref, q_ref, k_ref, v_ref, o_ref):
    i = pl.program_id(0)
    e0 = ends_ref[0]
    e1 = ends_ref[1]
    scale = 1.0 / math.sqrt(HEAD_DIM)

    def doc_start(t):
        return jnp.where(t >= e1, e1, jnp.where(t >= e0, e0, 0))

    q_lo = i * BQ
    j_lo = doc_start(q_lo) // BK
    j_hi = (q_lo + BQ - 1) // BK
    q = q_ref[...]
    q_pos = q_lo + lax.broadcasted_iota(jnp.int32, (BQ, 1), 0)
    q_start = doc_start(q_pos)

    def body(j, carry):
        m, l, acc = carry
        base = pl.multiple_of(j * BK, BK)
        k = k_ref[pl.ds(base, BK), :]
        v = v_ref[pl.ds(base, BK), :]
        s = lax.dot_general(
            q, k, (((1,), (1,)), ((), ())), preferred_element_type=jnp.float32
        ) * scale
        k_pos = base + lax.broadcasted_iota(jnp.int32, (1, BK), 1)
        mask = (k_pos <= q_pos) & (k_pos >= q_start)
        s = jnp.where(mask, s, -1e30)
        m_new = jnp.maximum(m, jnp.max(s, axis=1, keepdims=True))
        p = jnp.where(mask, jnp.exp(s - m_new), 0.0)
        alpha = jnp.exp(m - m_new)
        l = alpha * l + jnp.sum(p, axis=1, keepdims=True)
        acc = alpha * acc + jnp.dot(
            p.astype(jnp.bfloat16), v, preferred_element_type=jnp.float32
        )
        return m_new, l, acc

    carry = (
        jnp.full((BQ, 1), -1e30, jnp.float32),
        jnp.zeros((BQ, 1), jnp.float32),
        jnp.zeros((BQ, HEAD_DIM), jnp.float32),
    )
    m, l, acc = lax.fori_loop(j_lo, j_hi + 1, body, carry)
    o_ref[...] = (acc / l).astype(o_ref.dtype)

def attend(qkv, ends):
    seq = qkv.shape[1]

    def full(which):
        return pl.BlockSpec((None, seq, HEAD_DIM), lambda i, e: (which, 0, 0))

    return pl.pallas_call(
        flash_kernel,
        grid_spec=pltpu.PrefetchScalarGridSpec(
            num_scalar_prefetch=1,
            grid=(seq // BQ,),
            in_specs=[
                pl.BlockSpec((None, BQ, HEAD_DIM), lambda i, e: (0, i, 0)),
                full(1),
                full(2),
            ],
            out_specs=pl.BlockSpec((BQ, HEAD_DIM), lambda i, e: (i, 0)),
        ),
        out_shape=jax.ShapeDtypeStruct((seq, HEAD_DIM), jnp.bfloat16),
    )(ends, qkv, qkv, qkv)


def proj_kernel(mix_ref, att_ref, w_ref, o_ref, acc_ref, mixed_ref):
    i = pl.program_id(0)
    rows = w_ref.shape[0]
    cols = w_ref.shape[1]
    slots = rows // HEAD_DIM

    @pl.when(i == 0)
    def _():
        acc_ref[...] = jnp.zeros_like(acc_ref)

    w = w_ref[...]
    for b in range(PHM_N):
        for s in range(slots):
            part = att_ref[s].astype(jnp.float32) * mix_ref[(i * PHM_N + 0) * PHM_N + b]
            for a in range(1, PHM_N):
                part = part + att_ref[a * slots + s].astype(jnp.float32) * mix_ref[(i * PHM_N + a) * PHM_N + b]
            mixed_ref[:, s * HEAD_DIM:(s + 1) * HEAD_DIM] = part.astype(jnp.bfloat16)
        acc_ref[b] += jnp.dot(mixed_ref[...], w, preferred_element_type=jnp.float32)

    @pl.when(i == PHM_N - 1)
    def _():
        for b in range(PHM_N):
            o_ref[:, b * cols:(b + 1) * cols] = acc_ref[b].astype(o_ref.dtype)


def project(att, mix, w):
    heads, tok, _ = att.shape
    rows = heads * HEAD_DIM // PHM_N
    cols = w.shape[1]
    return pl.pallas_call(
        proj_kernel,
        grid=(PHM_N,),
        in_specs=[
            pl.BlockSpec(memory_space=pltpu.SMEM),
            pl.BlockSpec((heads, tok, HEAD_DIM), lambda i: (0, 0, 0)),
            pl.BlockSpec((rows, cols), lambda i: (i, 0)),
        ],
        out_specs=pl.BlockSpec((tok, PHM_N * cols), lambda i: (0, 0)),
        out_shape=jax.ShapeDtypeStruct((tok, PHM_N * cols), jnp.bfloat16),
        scratch_shapes=[
            pltpu.VMEM((PHM_N, tok, cols), jnp.float32),
            pltpu.VMEM((tok, rows), jnp.bfloat16),
        ],
    )(mix.reshape(-1), att, w)


def body(queries, key_rows, value_rows, doc_blocks, phm_mix, phm_blocks):
    tok_rows = queries.shape[0]
    heads = queries.shape[1] // HEAD_DIM
    factors = lax.all_gather(phm_blocks, "ctx", axis=0, tiled=True)
    stacked = jnp.stack(
        [x.reshape(tok_rows, heads, HEAD_DIM).transpose(1, 0, 2) for x in (queries, key_rows, value_rows)]
    )
    gathered = lax.all_to_all(stacked, "ctx", split_axis=1, concat_axis=1, tiled=True)
    seq_len = heads * tok_rows
    ends = jnp.cumsum(doc_blocks.astype(jnp.int32) * UNIT).astype(jnp.int32)
    attended = attend(gathered.reshape(3, seq_len, HEAD_DIM), ends)
    returned = lax.all_to_all(
        attended.reshape(heads, tok_rows, HEAD_DIM), "ctx", split_axis=0, concat_axis=0, tiled=True
    )
    return project(returned, phm_mix, factors)


def solution(mesh):
    rows = P(("rep", "ctx"), None)
    placed = (rows, rows, rows, P("rep"), P(), P("ctx", None))
    return jax.shard_map(body, mesh=mesh, in_specs=placed, out_specs=rows, check_vma=False)
```

time: 344 us -> 216 us (0.63)
  waiting for transfers between devices: 241 us -> 120 us
  local copies, waits for them, and re-layouts: 25.1 us -> 11.3 us
  Pallas kernels: 40.6 us -> 49.3 us
  starting transfers between devices: 15.9 us -> 20.1 us
    all_gather x3 -> x1, waiting for transfers between devices: 140 us -> 0.01 us  [body(): factors = lax.all_gather(phm_blocks, 'ctx', axis=0, tiled=True)]
    all_to_all x2, waiting for transfers between devices: 102 us -> 119 us  [the longest x1 90.8 us: body(): lax.all_to_all(stacked, 'ctx', split_axis=1, concat_axis=1, tiled=True)]
    transpose x1 -> x0, local copies, waits for them, and re-layouts: 9.43 us -> none  [gather_factors(): return over_core.transpose(2, 1, 0, 3, 4).reshape(-1, cols)]
    pallas_call x1, Pallas kernels: 30.5 us -> 37.5 us  [attend(): pl.pallas_call(flash_kernel, grid_spec=pltpu.PrefetchScalarGridSpec(num_s...]
    all_to_all x2, starting transfers between devices: 15.8 us -> 20.1 us  [the longest x1 11.6 us: body(): lax.all_to_all(stacked, 'ctx', split_axis=1, concat_axis=1, tiled=True)]
    unnamed x19 -> x13, local copies, waits for them, and re-layouts: 8.62 us -> 5.84 us
  transfers between devices with their start and end apart: 5 -> 3, of which waited for: 4 -> 2; matrix products, arithmetic and copies ran while one was open for 6% -> 6% of each run, Pallas kernels for 9% -> 17%
where the time goes in v3:
time: 216 us; the launch traced here: 217 us
  waiting for transfers between devices  120 us (56%)
  Pallas kernels  49.3 us (23%)
  starting transfers between devices  20.1 us (9%)
  between operations  13.4 us (6%)
  local copies, waits for them, and re-layouts  11.3 us (5%)
  other arithmetic  2.96 us (1%)
    all_to_all x1, waiting for transfers between devices, body(): lax.all_to_all(stacked, 'ctx', split_axis=1, concat_axis=1, tiled=True)  90.8 us
    pallas_call x1, Pallas kernels, attend(): pl.pallas_call(flash_kernel, grid_spec=pltpu.PrefetchScalarGridSpec(num_s...  37.5 us
    all_to_all x1, waiting for transfers between devices, body(): lax.all_to_all(attended.reshape(heads, tok_rows, HEAD_DIM), 'ctx', split_...  28 us
    pallas_call x1, Pallas kernels, project(): pl.pallas_call(proj_kernel, grid=(PHM_N,), in_specs=[pl.BlockSpec(memory_...  11.8 us
    all_to_all x1, starting transfers between devices, body(): lax.all_to_all(stacked, 'ctx', split_axis=1, concat_axis=1, tiled=True)  11.6 us
    all_to_all x1, starting transfers between devices, body(): lax.all_to_all(attended.reshape(heads, tok_rows, HEAD_DIM), 'ctx', split_...  8.5 us
    unnamed x13, local copies, waits for them, and re-layouts  5.84 us
  transfers between devices with their start and end apart: 3, of which 2 were waited for; matrix products, arithmetic and copies ran while one was open for 6% of the time, Pallas kernels for 17%

profile of v3, /device:TPU:2, one launch (start us, length us, event | category | flops | bytes accessed | tf_op | source)
XLA Modules:
  0.0 216.6 jit_solution(8986384385417907580)
XLA Ops:
  6.5 0.0 copy-start.1
  6.5 0.0 copy-start.2
  6.5 0.0 all-gather.2.cloned.1.call-start
  6.5 0.7 all-gather.2.cloned.1.call-update
  7.3 2.3 %copy.13 = bf16[128,4096]{0,1:T(8,128)(2,1)} copy(bf16[128,4096]{1,0:T(8,128)(2,1)} %param.8) | data formatting | bytes 2097152 | tf_op args[2]
  9.5 0.0 copy-done.1
  9.5 1.3 copy.11
  10.8 0.0 copy-done.2
  10.8 1.3 copy.12
  12.1 2.2 %pad_maximum_fusion = bf16[3,32,128,128]{2,3,1,0:T(8,128)(2,1)S(1)} fusion(bf16[1,32,128,128]{2,3,1,0:T(8,128)(2,1)} %bitcast.23, bf16[1,32,128,128]{2,3,1,0:T(8,128)(2,1)} %bitcast.25, bf16[1,32,128,128]{2,3,1,0:T(8,128)(2,1)} %bitcast.24), kind=kLoop, calls=%fused_computation | loop fusion | flops 3145728 | bytes 6291456 | tf_op jit(solution)/shard_map/stack | solution.py:134
  14.3 2.8 %copy.14 = bf16[3,32,128,128]{3,2,0,1:T(8,128)(2,1)} copy(bf16[3,32,128,128]{2,3,1,0:T(8,128)(2,1)S(1)} %pad_maximum_fusion) | data formatting | bytes 6291456 | tf_op jit(solution)/shard_map/stack | solution.py:134
  17.2 0.0 copy-start.4
  17.2 11.6 %all-to-all-start = ((bf16[3,32,128,128]{3,2,0,1:T(8,128)(2,1)}), bf16[3,32,128,128]{3,2,0,1:T(8,128)(2,1)S(1)}, u32[]{:S(2)}, u32[]{:S(2)}) async-start(bf16[3,32,128,128]{3,2,0,1:T(8,128)(2,1)} %copy.14), calls=%async_computation | async-start | bytes 6291456 | tf_op jit(solution)/shard_map/all_to_all | solution.py:137
  28.8 0.0 copy-done.4
  28.8 0.8 reduce-window.9
  29.6 90.8 %all-to-all-done = bf16[3,32,128,128]{3,2,0,1:T(8,128)(2,1)S(1)} async-done(((bf16[3,32,128,128]{3,2,0,1:T(8,128)(2,1)}), bf16[3,32,128,128]{3,2,0,1:T(8,128)(2,1)S(1)}, u32[]{:S(2)}, u32[]{:S(2)}) %all-to-all-start) | async-done | bytes 3145760 | tf_op jit(solution)/shard_map/all_to_all | solution.py:137
  120.4 2.0 copy.15
  122.4 0.0 copy-start.3
  122.4 37.5 %shard_map.64 = bf16[4096,128]{1,0:T(8,128)(2,1)} custom-call(s32[3]{0:T(128)} %bitcast.27, bf16[3,4096,128]{2,1,0:T(8,128)(2,1)} %bitcast.20, bf16[3,4096,128]{2,1,0:T(8,128)(2,1)} %bitcast.21, bf16[3,4096,128]{2,1,0:T(8,128)(2,1)} %bitcast.22), custom_call_target="tpu_custom_call" | custom-call | tf_op jit(solution)/shard_map/pallas_call | solution.py:68
  159.9 8.5 %all-to-all-start.1 = ((bf16[32,128,128]{2,1,0:T(8,128)(2,1)}), bf16[32,128,128]{2,1,0:T(8,128)(2,1)S(1)}, u32[]{:S(2)}, u32[]{:S(2)}) async-start(bf16[32,128,128]{2,1,0:T(8,128)(2,1)} %bitcast.26), calls=%async_computation.1 | async-start | bytes 2097152 | tf_op jit(solution)/shard_map/all_to_all | solution.py:141
  168.4 0.0 copy-done.3
  168.4 0.6 reshape.44.mix_ref
  169.0 28.0 %all-to-all-done.1.att_ref = bf16[32,128,128]{2,1,0:T(8,128)(2,1)S(1)} async-done(((bf16[32,128,128]{2,1,0:T(8,128)(2,1)}), bf16[32,128,128]{2,1,0:T(8,128)(2,1)S(1)}, u32[]{:S(2)}, u32[]{:S(2)}) %all-to-all-start.1) | async-done | bytes 1048608 | tf_op jit(solution)/shard_map/all_to_all | solution.py:141
  197.0 0.0 copy-start
  197.0 0.0 all-gather.2.cloned.1.call-done.w_ref
  197.0 1.0 copy-done
  198.0 11.8 %shard_map.65 = bf16[128,5120]{1,0:T(8,128)(2,1)} custom-call(f32[64]{0:T(128)} %reshape.44.mix_ref, bf16[32,128,128]{2,1,0:T(8,128)(2,1)} %copy-done, bf16[4096,1280]{1,0:T(8,128)(2,1)} %all-gather.2.cloned.1.call-done.w_ref), custom_call_target="tpu_custom_call" | custom-call | tf_op jit(solution)/shard_map/pallas_call | solution.py:113
  (1 shorter events, 0.0 us)
Async XLA Ops:
  6.5 3.0 %copy-start.1 = (bf16[128,4096]{1,0:T(8,128)(2,1)S(1)}, bf16[128,4096]{1,0:T(8,128)(2,1)}, u32[]{:S(2)}) copy-start(bf16[128,4096]{1,0:T(8,128)(2,1)} %param.6) | copy-start | bytes 3145732
  6.5 4.3 %copy-start.2 = (bf16[128,4096]{1,0:T(8,128)(2,1)S(1)}, bf16[128,4096]{1,0:T(8,128)(2,1)}, u32[]{:S(2)}) copy-start(bf16[128,4096]{1,0:T(8,128)(2,1)} %param.7) | copy-start | bytes 3145732
  6.5 190.5 %all-gather.2.cloned.1.call-start = ((), (), s32[]{:S(2)}) async-start(), calls=%async_computation.2 | async-start | bytes 10813440 | tf_op jit(solution)/shard_map/all_gather | solution.py:133
  17.2 11.6 %copy-start.4 = (s32[3]{0:T(128)S(1)}, s32[3]{0:T(128)}, u32[]{:S(2)}) copy-start(s32[3]{0:T(128)} %param.9) | copy-start | bytes 40
  17.2 103.2 %all-to-all-start = ((bf16[3,32,128,128]{3,2,0,1:T(8,128)(2,1)}), bf16[3,32,128,128]{3,2,0,1:T(8,128)(2,1)S(1)}, u32[]{:S(2)}, u32[]{:S(2)}) async-start(bf16[3,32,128,128]{3,2,0,1:T(8,128)(2,1)} %copy.14), calls=%async_computation | async-start | bytes 6291456 | tf_op jit(solution)/shard_map/all_to_all | solution.py:137
  122.4 46.0 %copy-start.3 = (f32[4,4,4]{2,1,0:T(4,128)S(1)}, f32[4,4,4]{2,1,0:T(4,128)}, u32[]{:S(2)}) copy-start(f32[4,4,4]{2,1,0:T(4,128)} %param.10) | copy-start | bytes 772
  159.9 37.1 %all-to-all-start.1 = ((bf16[32,128,128]{2,1,0:T(8,128)(2,1)}), bf16[32,128,128]{2,1,0:T(8,128)(2,1)S(1)}, u32[]{:S(2)}, u32[]{:S(2)}) async-start(bf16[32,128,128]{2,1,0:T(8,128)(2,1)} %bitcast.26), calls=%async_computation.1 | async-start | bytes 2097152 | tf_op jit(solution)/shard_map/all_to_all | solution.py:141
  197.0 1.0 copy-start
Sparse Core Ops, SparseCore 0:
  9.9 149.9 all-gather.1

commit v4 on v3

--- a/solution.py
+++ b/solution.py
@@ -20,30 +20,38 @@
     e0 = ends_ref[0]
     e1 = ends_ref[1]
     scale = 1.0 / math.sqrt(HEAD_DIM)
+    per = BK // UNIT
 
     def doc_start(t):
         return jnp.where(t >= e1, e1, jnp.where(t >= e0, e0, 0))
 
     q_lo = i * BQ
+    q_hi = q_lo + BQ - 1
     j_lo = doc_start(q_lo) // BK
-    j_hi = (q_lo + BQ - 1) // BK
-    q = q_ref[...]
+    j_hi = q_hi // BK
+    full_lo = (doc_start(q_hi) + BK - 1) // BK
+    full_hi = (q_lo + 1) // BK - 1
+    mid_lo = jnp.maximum(j_lo, jnp.minimum(full_lo, j_hi + 1))
+    mid_hi = jnp.maximum(mid_lo, full_hi + 1)
+    q = q_ref[...].reshape(BQ, HEAD_DIM)
     q_pos = q_lo + lax.broadcasted_iota(jnp.int32, (BQ, 1), 0)
     q_start = doc_start(q_pos)
 
-    def body(j, carry):
+    def step(j, carry, masked):
         m, l, acc = carry
-        base = pl.multiple_of(j * BK, BK)
-        k = k_ref[pl.ds(base, BK), :]
-        v = v_ref[pl.ds(base, BK), :]
+        k = k_ref[pl.ds(j * per, per)].reshape(BK, HEAD_DIM)
+        v = v_ref[pl.ds(j * per, per)].reshape(BK, HEAD_DIM)
         s = lax.dot_general(
             q, k, (((1,), (1,)), ((), ())), preferred_element_type=jnp.float32
         ) * scale
-        k_pos = base + lax.broadcasted_iota(jnp.int32, (1, BK), 1)
-        mask = (k_pos <= q_pos) & (k_pos >= q_start)
-        s = jnp.where(mask, s, -1e30)
+        if masked:
+            k_pos = j * BK + lax.broadcasted_iota(jnp.int32, (1, BK), 1)
+            mask = (k_pos <= q_pos) & (k_pos >= q_start)
+            s = jnp.where(mask, s, -1e30)
         m_new = jnp.maximum(m, jnp.max(s, axis=1, keepdims=True))
-        p = jnp.where(mask, jnp.exp(s - m_new), 0.0)
+        p = jnp.exp(s - m_new)
+        if masked:
+            p = jnp.where(mask, p, 0.0)
         alpha = jnp.exp(m - m_new)
         l = alpha * l + jnp.sum(p, axis=1, keepdims=True)
         acc = alpha * acc + jnp.dot(
@@ -56,14 +64,20 @@
         jnp.zeros((BQ, 1), jnp.float32),
         jnp.zeros((BQ, HEAD_DIM), jnp.float32),
     )
-    m, l, acc = lax.fori_loop(j_lo, j_hi + 1, body, carry)
+    edge = functools.partial(step, masked=True)
+    inner = functools.partial(step, masked=False)
+    carry = lax.fori_loop(j_lo, mid_lo, edge, carry)
+    carry = lax.fori_loop(mid_lo, mid_hi, inner, carry)
+    m, l, acc = lax.fori_loop(mid_hi, j_hi + 1, edge, carry)
     o_ref[...] = (acc / l).astype(o_ref.dtype)
 
+
 def attend(qkv, ends):
-    seq = qkv.shape[1]
+    blocks = qkv.shape[0]
+    seq = blocks * UNIT
 
-    def full(which):
-        return pl.BlockSpec((None, seq, HEAD_DIM), lambda i, e: (which, 0, 0))
+    def whole(which):
+        return pl.BlockSpec((blocks, None, UNIT, HEAD_DIM), lambda i, e: (0, which, 0, 0))
 
     return pl.pallas_call(
         flash_kernel,
@@ -71,14 +85,35 @@
             num_scalar_prefetch=1,
             grid=(seq // BQ,),
             in_specs=[
-                pl.BlockSpec((None, BQ, HEAD_DIM), lambda i, e: (0, i, 0)),
-                full(1),
-                full(2),
+                pl.BlockSpec((BQ // UNIT, None, UNIT, HEAD_DIM), lambda i, e: (i, 0, 0, 0)),
+                whole(1),
+                whole(2),
             ],
             out_specs=pl.BlockSpec((BQ, HEAD_DIM), lambda i, e: (i, 0)),
         ),
         out_shape=jax.ShapeDtypeStruct((seq, HEAD_DIM), jnp.bfloat16),
     )(ends, qkv, qkv, qkv)
+
+
+def pack_kernel(q_ref, k_ref, v_ref, o_ref):
+    for h in range(o_ref.shape[0]):
+        for w, x_ref in enumerate((q_ref, k_ref, v_ref)):
+            o_ref[h, w] = x_ref[:, h * HEAD_DIM:(h + 1) * HEAD_DIM]
+
+
+def pack(queries, key_rows, value_rows):
+    tok, width = queries.shape
+    heads = width // HEAD_DIM
+    groups = 4
+    per = heads // groups
+    spec = pl.BlockSpec((tok, per * HEAD_DIM), lambda g: (0, g))
+    return pl.pallas_call(
+        pack_kernel,
+        grid=(groups,),
+        in_specs=[spec, spec, spec],
+        out_specs=pl.BlockSpec((per, 3, tok, HEAD_DIM), lambda g: (g, 0, 0, 0)),
+        out_shape=jax.ShapeDtypeStruct((heads, 3, tok, HEAD_DIM), queries.dtype),
+    )(queries, key_rows, value_rows)
 
 
 def proj_kernel(mix_ref, att_ref, w_ref, o_ref, acc_ref, mixed_ref):
@@ -131,13 +166,11 @@
     tok_rows = queries.shape[0]
     heads = queries.shape[1] // HEAD_DIM
     factors = lax.all_gather(phm_blocks, "ctx", axis=0, tiled=True)
-    stacked = jnp.stack(
-        [x.reshape(tok_rows, heads, HEAD_DIM).transpose(1, 0, 2) for x in (queries, key_rows, value_rows)]
-    )
-    gathered = lax.all_to_all(stacked, "ctx", split_axis=1, concat_axis=1, tiled=True)
+    stacked = pack(queries, key_rows, value_rows)
+    gathered = lax.all_to_all(stacked, "ctx", split_axis=0, concat_axis=0, tiled=True)
     seq_len = heads * tok_rows
     ends = jnp.cumsum(doc_blocks.astype(jnp.int32) * UNIT).astype(jnp.int32)
-    attended = attend(gathered.reshape(3, seq_len, HEAD_DIM), ends)
+    attended = attend(gathered, ends)
     returned = lax.all_to_all(
         attended.reshape(heads, tok_rows, HEAD_DIM), "ctx", split_axis=0, concat_axis=0, tiled=True
     )

time: 216 us -> 207 us (0.958)
  the two profiles are of different devices: /device:TPU:2 before, /device:TPU:39 now
where the time goes in v4:
time: 207 us; the launch traced here: 206 us
  waiting for transfers between devices  118 us (57%)
  Pallas kernels  52.4 us (25%)
  starting transfers between devices  18.2 us (9%)
  between operations  13.4 us (6%)
  local copies, waits for them, and re-layouts  3.42 us (2%)
    all_to_all x1, waiting for transfers between devices, body(): lax.all_to_all(stacked, 'ctx', split_axis=0, concat_axis=0, tiled=True)  89.8 us
    pallas_call x1, Pallas kernels, attend(): pl.pallas_call(flash_kernel, grid_spec=pltpu.PrefetchScalarGridSpec(num_s...  36.1 us
    all_to_all x1, waiting for transfers between devices, body(): lax.all_to_all(attended.reshape(heads, tok_rows, HEAD_DIM), 'ctx', split_...  27.6 us
    pallas_call x1, Pallas kernels, project(): pl.pallas_call(proj_kernel, grid=(PHM_N,), in_specs=[pl.BlockSpec(memory_...  11.9 us
    all_to_all x1, starting transfers between devices, body(): lax.all_to_all(stacked, 'ctx', split_axis=0, concat_axis=0, tiled=True)  10.9 us
    all_to_all x1, starting transfers between devices, body(): lax.all_to_all(attended.reshape(heads, tok_rows, HEAD_DIM), 'ctx', split_...  7.26 us
    pallas_call x1, Pallas kernels, pack(): pl.pallas_call(pack_kernel, grid=(groups,), in_specs=[spec, spec, spec],...  4.38 us
  transfers between devices with their start and end apart: 3, of which 2 were waited for; matrix products, arithmetic and copies ran while one was open for 1% of the time, Pallas kernels for 20%

profile of v4, /device:TPU:39, one launch (start us, length us, event | category | flops | bytes accessed | tf_op | source)
XLA Modules:
  0.0 206.2 jit_solution(17412334415431996540)
XLA Ops:
  6.5 0.0 all-gather.2.cloned.1.call-start
  6.5 0.7 all-gather.2.cloned.1.call-update
  7.3 4.4 %shard_map.64 = bf16[32,3,128,128]{3,2,1,0:T(8,128)(2,1)} custom-call(bf16[128,4096]{1,0:T(8,128)(2,1)} %q_ref.1, bf16[128,4096]{1,0:T(8,128)(2,1)} %k_ref.1, bf16[128,4096]{1,0:T(8,128)(2,1)} %v_ref.1), custom_call_target="tpu_custom_call" | custom-call | tf_op jit(solution)/shard_map/pallas_call | solution.py:110
  11.6 0.0 copy-start.3
  11.6 10.9 %all-to-all-start = ((bf16[32,3,128,128]{3,2,1,0:T(8,128)(2,1)}), bf16[32,3,128,128]{3,2,1,0:T(8,128)(2,1)S(1)}, u32[]{:S(2)}, u32[]{:S(2)}) async-start(bf16[32,3,128,128]{3,2,1,0:T(8,128)(2,1)} %shard_map.64), calls=%async_computation | async-start | bytes 6291456 | tf_op jit(solution)/shard_map/all_to_all | solution.py:170
  22.6 0.0 copy-done.3
  22.6 0.7 reduce-window.9
  23.3 89.8 %all-to-all-done.q_ref.k_ref.v_ref = bf16[32,3,128,128]{3,2,1,0:T(8,128)(2,1)S(1)} async-done(((bf16[32,3,128,128]{3,2,1,0:T(8,128)(2,1)}), bf16[32,3,128,128]{3,2,1,0:T(8,128)(2,1)S(1)}, u32[]{:S(2)}, u32[]{:S(2)}) %all-to-all-start) | async-done | bytes 3145760 | tf_op jit(solution)/shard_map/all_to_all | solution.py:170
  113.1 0.0 copy-start
  113.1 1.7 copy-done
  114.9 0.0 copy-start.2
  114.9 36.1 %shard_map.65 = bf16[4096,128]{1,0:T(8,128)(2,1)} custom-call(s32[3]{0:T(128)} %bitcast.5, bf16[32,3,128,128]{3,2,1,0:T(8,128)(2,1)} %copy-done, bf16[32,3,128,128]{3,2,1,0:T(8,128)(2,1)} %copy-done, bf16[32,3,128,128]{3,2,1,0:T(8,128)(2,1)} %copy-done), custom_call_target="tpu_custom_call" | custom-call | tf_op jit(solution)/shard_map/pallas_call | solution.py:82
  151.0 7.3 %all-to-all-start.1 = ((bf16[32,128,128]{2,1,0:T(8,128)(2,1)}), bf16[32,128,128]{2,1,0:T(8,128)(2,1)S(1)}, u32[]{:S(2)}, u32[]{:S(2)}) async-start(bf16[32,128,128]{2,1,0:T(8,128)(2,1)} %bitcast.4), calls=%async_computation.1 | async-start | bytes 2097152 | tf_op jit(solution)/shard_map/all_to_all | solution.py:174
  158.3 0.0 copy-done.2
  158.3 0.7 reshape.32.mix_ref
  159.0 27.6 %all-to-all-done.1.att_ref = bf16[32,128,128]{2,1,0:T(8,128)(2,1)S(1)} async-done(((bf16[32,128,128]{2,1,0:T(8,128)(2,1)}), bf16[32,128,128]{2,1,0:T(8,128)(2,1)S(1)}, u32[]{:S(2)}, u32[]{:S(2)}) %all-to-all-start.1) | async-done | bytes 1048608 | tf_op jit(solution)/shard_map/all_to_all | solution.py:174
  186.5 0.0 copy-start.1
  186.5 0.0 all-gather.2.cloned.1.call-done.w_ref
  186.6 1.0 copy-done.1
  187.5 11.9 %shard_map.66 = bf16[128,5120]{1,0:T(8,128)(2,1)} custom-call(f32[64]{0:T(128)} %reshape.32.mix_ref, bf16[32,128,128]{2,1,0:T(8,128)(2,1)} %copy-done.1, bf16[4096,1280]{1,0:T(8,128)(2,1)} %all-gather.2.cloned.1.call-done.w_ref), custom_call_target="tpu_custom_call" | custom-call | tf_op jit(solution)/shard_map/pallas_call | solution.py:148
  (1 shorter events, 0.0 us)
Async XLA Ops:
  6.5 180.0 %all-gather.2.cloned.1.call-start = ((), (), s32[]{:S(2)}) async-start(), calls=%async_computation.2 | async-start | bytes 10813440 | tf_op jit(solution)/shard_map/all_gather | solution.py:168
  11.6 10.9 %copy-start.3 = (s32[3]{0:T(128)S(1)}, s32[3]{0:T(128)}, u32[]{:S(2)}) copy-start(s32[3]{0:T(128)} %param.9) | copy-start | bytes 40
  11.6 101.5 %all-to-all-start = ((bf16[32,3,128,128]{3,2,1,0:T(8,128)(2,1)}), bf16[32,3,128,128]{3,2,1,0:T(8,128)(2,1)S(1)}, u32[]{:S(2)}, u32[]{:S(2)}) async-start(bf16[32,3,128,128]{3,2,1,0:T(8,128)(2,1)} %shard_map.64), calls=%async_computation | async-start | bytes 6291456 | tf_op jit(solution)/shard_map/all_to_all | solution.py:170
  113.1 1.7 copy-start
  114.9 43.4 %copy-start.2 = (f32[4,4,4]{2,1,0:T(4,128)S(1)}, f32[4,4,4]{2,1,0:T(4,128)}, u32[]{:S(2)}) copy-start(f32[4,4,4]{2,1,0:T(4,128)} %param.10) | copy-start | bytes 772
  151.0 35.5 %all-to-all-start.1 = ((bf16[32,128,128]{2,1,0:T(8,128)(2,1)}), bf16[32,128,128]{2,1,0:T(8,128)(2,1)S(1)}, u32[]{:S(2)}, u32[]{:S(2)}) async-start(bf16[32,128,128]{2,1,0:T(8,128)(2,1)} %bitcast.4), calls=%async_computation.1 | async-start | bytes 2097152 | tf_op jit(solution)/shard_map/all_to_all | solution.py:174
  186.5 1.0 copy-start.1
Sparse Core Ops, SparseCore 0:
  9.9 144.7 all-gather.1

commit v5 on v4

--- a/solution.py
+++ b/solution.py
@@ -7,6 +7,7 @@
 from jax.experimental import pallas as pl
 from jax.experimental.pallas import tpu as pltpu
 from jax.sharding import PartitionSpec as P
+
 
 HEAD_DIM = 128
 PHM_N = 4
@@ -68,7 +69,7 @@
     inner = functools.partial(step, masked=False)
     carry = lax.fori_loop(j_lo, mid_lo, edge, carry)
     carry = lax.fori_loop(mid_lo, mid_hi, inner, carry)
-    m, l, acc = lax.fori_loop(mid_hi, j_hi + 1, edge, carry)
+    _, l, acc = lax.fori_loop(mid_hi, j_hi + 1, edge, carry)
     o_ref[...] = (acc / l).astype(o_ref.dtype)
 
 
@@ -118,22 +119,25 @@
 
 def proj_kernel(mix_ref, att_ref, w_ref, o_ref, acc_ref, mixed_ref):
     i = pl.program_id(0)
-    rows = w_ref.shape[0]
-    cols = w_ref.shape[1]
+    halves, rows, half_cols = w_ref.shape
+    cols = halves * half_cols
     slots = rows // HEAD_DIM
 
     @pl.when(i == 0)
     def _():
         acc_ref[...] = jnp.zeros_like(acc_ref)
 
-    w = w_ref[...]
     for b in range(PHM_N):
         for s in range(slots):
             part = att_ref[s].astype(jnp.float32) * mix_ref[(i * PHM_N + 0) * PHM_N + b]
             for a in range(1, PHM_N):
                 part = part + att_ref[a * slots + s].astype(jnp.float32) * mix_ref[(i * PHM_N + a) * PHM_N + b]
             mixed_ref[:, s * HEAD_DIM:(s + 1) * HEAD_DIM] = part.astype(jnp.bfloat16)
-        acc_ref[b] += jnp.dot(mixed_ref[...], w, preferred_element_type=jnp.float32)
+        mixed = mixed_ref[...]
+        for h in range(halves):
+            acc_ref[b, :, h * half_cols:(h + 1) * half_cols] += jnp.dot(
+                mixed, w_ref[h], preferred_element_type=jnp.float32
+            )
 
     @pl.when(i == PHM_N - 1)
     def _():
@@ -143,15 +147,16 @@
 
 def project(att, mix, w):
     heads, tok, _ = att.shape
+    halves, _, half_cols = w.shape
     rows = heads * HEAD_DIM // PHM_N
-    cols = w.shape[1]
+    cols = halves * half_cols
     return pl.pallas_call(
         proj_kernel,
         grid=(PHM_N,),
         in_specs=[
             pl.BlockSpec(memory_space=pltpu.SMEM),
             pl.BlockSpec((heads, tok, HEAD_DIM), lambda i: (0, 0, 0)),
-            pl.BlockSpec((rows, cols), lambda i: (i, 0)),
+            pl.BlockSpec((halves, rows, half_cols), lambda i: (0, i, 0)),
         ],
         out_specs=pl.BlockSpec((tok, PHM_N * cols), lambda i: (0, 0)),
         out_shape=jax.ShapeDtypeStruct((tok, PHM_N * cols), jnp.bfloat16),
@@ -162,13 +167,20 @@
     )(mix.reshape(-1), att, w)
 
 
+def gather_factors(phm_blocks):
+    cols = phm_blocks.shape[1]
+    half = cols // lax.axis_size("core")
+    mine = lax.dynamic_slice_in_dim(phm_blocks, lax.axis_index("core") * half, half, 1)
+    over_ctx = lax.all_gather(mine, "ctx", axis=0, tiled=True)
+    return lax.all_gather(over_ctx, "core", axis=0)
+
+
 def body(queries, key_rows, value_rows, doc_blocks, phm_mix, phm_blocks):
     tok_rows = queries.shape[0]
     heads = queries.shape[1] // HEAD_DIM
-    factors = lax.all_gather(phm_blocks, "ctx", axis=0, tiled=True)
+    factors = gather_factors(phm_blocks)
     stacked = pack(queries, key_rows, value_rows)
     gathered = lax.all_to_all(stacked, "ctx", split_axis=0, concat_axis=0, tiled=True)
-    seq_len = heads * tok_rows
     ends = jnp.cumsum(doc_blocks.astype(jnp.int32) * UNIT).astype(jnp.int32)
     attended = attend(gathered, ends)
     returned = lax.all_to_all(
@@ -178,6 +190,12 @@
 
 
 def solution(mesh):
-    rows = P(("rep", "ctx"), None)
-    placed = (rows, rows, rows, P("rep"), P(), P("ctx", None))
-    return jax.shard_map(body, mesh=mesh, in_specs=placed, out_specs=rows, check_vma=False)
+    rep_at = mesh.axis_names.index("rep")
+    shape = list(mesh.devices.shape)
+    shape[rep_at:rep_at + 1] = [shape[rep_at] // 2, 2]
+    names = list(mesh.axis_names)
+    names[rep_at:rep_at + 1] = ["x", "core"]
+    split = jax.sharding.Mesh(mesh.devices.reshape(shape), tuple(names))
+    rows = P(("x", "core", "ctx"), None)
+    placed = (rows, rows, rows, P(("x", "core")), P(), P("ctx", None))
+    return jax.shard_map(body, mesh=split, in_specs=placed, out_specs=rows, check_vma=False)

time: 207 us -> 271 us (1.31)
  the two profiles are of different devices: /device:TPU:39 before, /device:TPU:2 now
where the time goes in v5:
time: 271 us; the launch traced here: 269 us
  waiting for transfers between devices  188 us (69%)
  Pallas kernels  51.5 us (19%)
  between operations  13.4 us (5%)
  starting transfers between devices  9.81 us (4%)
  local copies, waits for them, and re-layouts  4.95 us (2%)
    all_gather x1, waiting for transfers between devices, gather_factors(): over_ctx = lax.all_gather(mine, 'ctx', axis=0, tiled=True)  89.5 us
    all_to_all x1, waiting for transfers between devices, body(): lax.all_to_all(stacked, 'ctx', split_axis=0, concat_axis=0, tiled=True)  71.1 us
    pallas_call x1, Pallas kernels, attend(): pl.pallas_call(flash_kernel, grid_spec=pltpu.PrefetchScalarGridSpec(num_s...  34.2 us
    all_to_all x1, waiting for transfers between devices, body(): lax.all_to_all(attended.reshape(heads, tok_rows, HEAD_DIM), 'ctx', split_...  27.5 us
    pallas_call x1, Pallas kernels, project(): pl.pallas_call(proj_kernel, grid=(PHM_N,), in_specs=[pl.BlockSpec(memory_...  12.9 us
    all_to_all x1, starting transfers between devices, body(): lax.all_to_all(stacked, 'ctx', split_axis=0, concat_axis=0, tiled=True)  5.72 us
  transfers between devices with their start and end apart: 4, of which 3 were waited for; matrix products, arithmetic and copies ran while one was open for 1% of the time, Pallas kernels for 14%

profile of v5, /device:TPU:2, one launch (start us, length us, event | category | flops | bytes accessed | tf_op | source)
XLA Modules:
  0.0 268.7 jit_solution(11527899013315812637)
XLA Ops:
  6.5 0.0 copy-start
  6.5 0.0 all-gather.4.cloned.1.call-start
  6.5 1.0 copy-done
  7.5 0.7 constant_dynamic-slice_fusion
  8.2 0.0 all-gather.4.cloned.1.call-update
  8.2 0.0 all-gather.6.cloned.1.call-start
  8.3 89.5 %all-gather.4.cloned.1.call-done = bf16[4096,640]{1,0:T(8,128)(2,1)} async-done(((bf16[128,640]{1,0:T(8,128)(2,1)}), bf16[4096,640]{1,0:T(8,128)(2,1)}) %all-gather.4.cloned.1.call-update) | async-done | bytes 5242896 | tf_op jit(solution)/shard_map/all_gather | solution.py:174
  97.8 0.0 all-gather.6.cloned.1.call-update
  97.8 4.4 %shard_map.64 = bf16[32,3,128,128]{3,2,1,0:T(8,128)(2,1)} custom-call(bf16[128,4096]{1,0:T(8,128)(2,1)} %q_ref.1, bf16[128,4096]{1,0:T(8,128)(2,1)} %k_ref.1, bf16[128,4096]{1,0:T(8,128)(2,1)} %v_ref.1), custom_call_target="tpu_custom_call" | custom-call | tf_op jit(solution)/shard_map/pallas_call | solution.py:111
  102.2 0.0 copy-start.4
  102.2 5.7 %all-to-all-start = ((bf16[32,3,128,128]{3,2,1,0:T(8,128)(2,1)}), bf16[32,3,128,128]{3,2,1,0:T(8,128)(2,1)S(1)}, u32[]{:S(2)}, u32[]{:S(2)}) async-start(bf16[32,3,128,128]{3,2,1,0:T(8,128)(2,1)} %shard_map.64), calls=%async_computation | async-start | bytes 6291456 | tf_op jit(solution)/shard_map/all_to_all | solution.py:183
  108.0 0.0 copy-done.4
  108.0 0.7 reduce-window.9
  108.7 71.1 %all-to-all-done.q_ref.k_ref.v_ref = bf16[32,3,128,128]{3,2,1,0:T(8,128)(2,1)S(1)} async-done(((bf16[32,3,128,128]{3,2,1,0:T(8,128)(2,1)}), bf16[32,3,128,128]{3,2,1,0:T(8,128)(2,1)S(1)}, u32[]{:S(2)}, u32[]{:S(2)}) %all-to-all-start) | async-done | bytes 3145760 | tf_op jit(solution)/shard_map/all_to_all | solution.py:183
  179.8 0.0 copy-start.1
  179.8 1.6 copy-done.1
  181.4 0.0 copy-start.3
  181.4 34.2 %shard_map.65 = bf16[4096,128]{1,0:T(8,128)(2,1)} custom-call(s32[3]{0:T(128)} %bitcast.7, bf16[32,3,128,128]{3,2,1,0:T(8,128)(2,1)} %copy-done.1, bf16[32,3,128,128]{3,2,1,0:T(8,128)(2,1)} %copy-done.1, bf16[32,3,128,128]{3,2,1,0:T(8,128)(2,1)} %copy-done.1), custom_call_target="tpu_custom_call" | custom-call | tf_op jit(solution)/shard_map/pallas_call | solution.py:83
  215.7 4.0 %all-to-all-start.1 = ((bf16[32,128,128]{2,1,0:T(8,128)(2,1)}), bf16[32,128,128]{2,1,0:T(8,128)(2,1)S(1)}, u32[]{:S(2)}, u32[]{:S(2)}) async-start(bf16[32,128,128]{2,1,0:T(8,128)(2,1)} %bitcast.6), calls=%async_computation.1 | async-start | bytes 2097152 | tf_op jit(solution)/shard_map/all_to_all | solution.py:186
  219.7 0.0 copy-done.3
  219.7 0.7 reshape.32.mix_ref
  220.4 27.5 %all-to-all-done.1.att_ref = bf16[32,128,128]{2,1,0:T(8,128)(2,1)S(1)} async-done(((bf16[32,128,128]{2,1,0:T(8,128)(2,1)}), bf16[32,128,128]{2,1,0:T(8,128)(2,1)S(1)}, u32[]{:S(2)}, u32[]{:S(2)}) %all-to-all-start.1) | async-done | bytes 1048608 | tf_op jit(solution)/shard_map/all_to_all | solution.py:186
  248.0 0.0 copy-start.2
  248.0 0.0 all-gather.6.cloned.1.call-done
  248.0 1.0 copy-done.2
  248.9 12.9 %shard_map.66 = bf16[128,5120]{1,0:T(8,128)(2,1)} custom-call(f32[64]{0:T(128)} %reshape.32.mix_ref, bf16[32,128,128]{2,1,0:T(8,128)(2,1)} %copy-done.2, bf16[2,4096,640]{2,1,0:T(8,128)(2,1)} %bitcast.5), custom_call_target="tpu_custom_call" | custom-call | tf_op jit(solution)/shard_map/pallas_call | solution.py:153
  (1 shorter events, 0.0 us)
Async XLA Ops:
  6.5 1.0 copy-start
  6.5 91.3 %all-gather.4.cloned.1.call-start = ((), (), s32[]{:S(2)}) async-start(), calls=%async_computation.2 | async-start | bytes 5406720 | tf_op jit(solution)/shard_map/all_gather | solution.py:174
  8.2 239.8 %all-gather.6.cloned.1.call-start = ((), (), s32[]{:S(2)}) async-start(), calls=%async_computation.3 | async-start | bytes 15728640 | tf_op jit(solution)/shard_map/all_gather | solution.py:175
  102.2 5.7 %copy-start.4 = (s32[3]{0:T(128)S(1)}, s32[3]{0:T(128)}, u32[]{:S(2)}) copy-start(s32[3]{0:T(128)} %param.9) | copy-start | bytes 40
  102.2 77.6 %all-to-all-start = ((bf16[32,3,128,128]{3,2,1,0:T(8,128)(2,1)}), bf16[32,3,128,128]{3,2,1,0:T(8,128)(2,1)S(1)}, u32[]{:S(2)}, u32[]{:S(2)}) async-start(bf16[32,3,128,128]{3,2,1,0:T(8,128)(2,1)} %shard_map.64), calls=%async_computation | async-start | bytes 6291456 | tf_op jit(solution)/shard_map/all_to_all | solution.py:183
  179.8 1.6 copy-start.1
  181.4 38.3 %copy-start.3 = (f32[4,4,4]{2,1,0:T(4,128)S(1)}, f32[4,4,4]{2,1,0:T(4,128)}, u32[]{:S(2)}) copy-start(f32[4,4,4]{2,1,0:T(4,128)} %param.10) | copy-start | bytes 772
  215.7 32.3 %all-to-all-start.1 = ((bf16[32,128,128]{2,1,0:T(8,128)(2,1)}), bf16[32,128,128]{2,1,0:T(8,128)(2,1)S(1)}, u32[]{:S(2)}, u32[]{:S(2)}) async-start(bf16[32,128,128]{2,1,0:T(8,128)(2,1)} %bitcast.6), calls=%async_computation.1 | async-start | bytes 2097152 | tf_op jit(solution)/shard_map/all_to_all | solution.py:186
  248.0 1.0 copy-start.2
Sparse Core Ops, SparseCore 0:
  9.9 87.8 all-gather.3
  99.6 25.0 all-gather.5

commit v6 on v5

--- a/solution.py
+++ b/solution.py
@@ -12,7 +12,7 @@
 HEAD_DIM = 128
 PHM_N = 4
 UNIT = 128
-BQ = 256
+BQ = 512
 BK = 256
 
 
@@ -117,7 +117,7 @@
     )(queries, key_rows, value_rows)
 
 
-def proj_kernel(mix_ref, att_ref, w_ref, o_ref, acc_ref, mixed_ref):
+def proj_kernel(mix_ref, att_ref, w_ref, o_ref, acc_ref, mixed_ref, wide_ref):
     i = pl.program_id(0)
     halves, rows, half_cols = w_ref.shape
     cols = halves * half_cols
@@ -126,12 +126,14 @@
     @pl.when(i == 0)
     def _():
         acc_ref[...] = jnp.zeros_like(acc_ref)
+        for h in range(att_ref.shape[0]):
+            wide_ref[h] = att_ref[h].astype(jnp.float32)
 
     for b in range(PHM_N):
         for s in range(slots):
-            part = att_ref[s].astype(jnp.float32) * mix_ref[(i * PHM_N + 0) * PHM_N + b]
+            part = wide_ref[s] * mix_ref[(i * PHM_N + 0) * PHM_N + b]
             for a in range(1, PHM_N):
-                part = part + att_ref[a * slots + s].astype(jnp.float32) * mix_ref[(i * PHM_N + a) * PHM_N + b]
+                part = part + wide_ref[a * slots + s] * mix_ref[(i * PHM_N + a) * PHM_N + b]
             mixed_ref[:, s * HEAD_DIM:(s + 1) * HEAD_DIM] = part.astype(jnp.bfloat16)
         mixed = mixed_ref[...]
         for h in range(halves):
@@ -163,6 +165,7 @@
         scratch_shapes=[
             pltpu.VMEM((PHM_N, tok, cols), jnp.float32),
             pltpu.VMEM((tok, rows), jnp.bfloat16),
+            pltpu.VMEM((heads, tok, HEAD_DIM), jnp.float32),
         ],
     )(mix.reshape(-1), att, w)
 

time: 271 us -> 263 us (0.970)
  Pallas kernels: 51.5 us -> 44 us
    pallas_call x1, Pallas kernels: 34.2 us -> 27 us  [attend(): pl.pallas_call(flash_kernel, grid_spec=pltpu.PrefetchScalarGridSpec(num_s...]
  transfers between devices with their start and end apart: 4 -> 4, of which waited for: 3 -> 3; matrix products, arithmetic and copies ran while one was open for 1% -> 1% of each run, Pallas kernels for 14% -> 12%
where the time goes in v6:
time: 263 us; the launch traced here: 262 us
  waiting for transfers between devices  189 us (72%)
  Pallas kernels  44 us (17%)
  between operations  13.4 us (5%)
  starting transfers between devices  9.81 us (4%)
  local copies, waits for them, and re-layouts  4.95 us (2%)
    all_gather x1, waiting for transfers between devices, gather_factors(): over_ctx = lax.all_gather(mine, 'ctx', axis=0, tiled=True)  89.5 us
    all_to_all x1, waiting for transfers between devices, body(): lax.all_to_all(stacked, 'ctx', split_axis=0, concat_axis=0, tiled=True)  71.1 us
    all_to_all x1, waiting for transfers between devices, body(): lax.all_to_all(attended.reshape(heads, tok_rows, HEAD_DIM), 'ctx', split_...  28.7 us
    pallas_call x1, Pallas kernels, attend(): pl.pallas_call(flash_kernel, grid_spec=pltpu.PrefetchScalarGridSpec(num_s...  27 us
    pallas_call x1, Pallas kernels, project(): pl.pallas_call(proj_kernel, grid=(PHM_N,), in_specs=[pl.BlockSpec(memory_...  12.6 us
    all_to_all x1, starting transfers between devices, body(): lax.all_to_all(stacked, 'ctx', split_axis=0, concat_axis=0, tiled=True)  5.72 us
  transfers between devices with their start and end apart: 4, of which 3 were waited for; matrix products, arithmetic and copies ran while one was open for 1% of the time, Pallas kernels for 12%

profile of v6, /device:TPU:2, one launch (start us, length us, event | category | flops | bytes accessed | tf_op | source)
XLA Modules:
  0.0 262.2 jit_solution(11941429300754729941)
XLA Ops:
  6.5 0.0 copy-start
  6.5 0.0 all-gather.4.cloned.1.call-start
  6.5 1.0 copy-done
  7.5 0.7 constant_dynamic-slice_fusion
  8.2 0.0 all-gather.4.cloned.1.call-update
  8.2 0.0 all-gather.6.cloned.1.call-start
  8.3 89.5 %all-gather.4.cloned.1.call-done = bf16[4096,640]{1,0:T(8,128)(2,1)} async-done(((bf16[128,640]{1,0:T(8,128)(2,1)}), bf16[4096,640]{1,0:T(8,128)(2,1)}) %all-gather.4.cloned.1.call-update) | async-done | bytes 5242896 | tf_op jit(solution)/shard_map/all_gather | solution.py:177
  97.8 0.0 all-gather.6.cloned.1.call-update
  97.8 4.4 %shard_map.64 = bf16[32,3,128,128]{3,2,1,0:T(8,128)(2,1)} custom-call(bf16[128,4096]{1,0:T(8,128)(2,1)} %q_ref.1, bf16[128,4096]{1,0:T(8,128)(2,1)} %k_ref.1, bf16[128,4096]{1,0:T(8,128)(2,1)} %v_ref.1), custom_call_target="tpu_custom_call" | custom-call | tf_op jit(solution)/shard_map/pallas_call | solution.py:111
  102.2 0.0 copy-start.4
  102.2 5.7 %all-to-all-start = ((bf16[32,3,128,128]{3,2,1,0:T(8,128)(2,1)}), bf16[32,3,128,128]{3,2,1,0:T(8,128)(2,1)S(1)}, u32[]{:S(2)}, u32[]{:S(2)}) async-start(bf16[32,3,128,128]{3,2,1,0:T(8,128)(2,1)} %shard_map.64), calls=%async_computation | async-start | bytes 6291456 | tf_op jit(solution)/shard_map/all_to_all | solution.py:186
  108.0 0.0 copy-done.4
  108.0 0.7 reduce-window.9
  108.7 71.1 %all-to-all-done.q_ref.k_ref.v_ref = bf16[32,3,128,128]{3,2,1,0:T(8,128)(2,1)S(1)} async-done(((bf16[32,3,128,128]{3,2,1,0:T(8,128)(2,1)}), bf16[32,3,128,128]{3,2,1,0:T(8,128)(2,1)S(1)}, u32[]{:S(2)}, u32[]{:S(2)}) %all-to-all-start) | async-done | bytes 3145760 | tf_op jit(solution)/shard_map/all_to_all | solution.py:186
  179.8 0.0 copy-start.1
  179.8 1.6 copy-done.1
  181.4 0.0 copy-start.3
  181.4 27.0 %shard_map.65 = bf16[4096,128]{1,0:T(8,128)(2,1)} custom-call(s32[3]{0:T(128)} %bitcast.7, bf16[32,3,128,128]{3,2,1,0:T(8,128)(2,1)} %copy-done.1, bf16[32,3,128,128]{3,2,1,0:T(8,128)(2,1)} %copy-done.1, bf16[32,3,128,128]{3,2,1,0:T(8,128)(2,1)} %copy-done.1), custom_call_target="tpu_custom_call" | custom-call | tf_op jit(solution)/shard_map/pallas_call | solution.py:83
  208.4 4.0 %all-to-all-start.1 = ((bf16[32,128,128]{2,1,0:T(8,128)(2,1)}), bf16[32,128,128]{2,1,0:T(8,128)(2,1)S(1)}, u32[]{:S(2)}, u32[]{:S(2)}) async-start(bf16[32,128,128]{2,1,0:T(8,128)(2,1)} %bitcast.6), calls=%async_computation.1 | async-start | bytes 2097152 | tf_op jit(solution)/shard_map/all_to_all | solution.py:189
  212.5 0.0 copy-done.3
  212.5 0.7 reshape.32.mix_ref
  213.1 28.7 %all-to-all-done.1.att_ref = bf16[32,128,128]{2,1,0:T(8,128)(2,1)S(1)} async-done(((bf16[32,128,128]{2,1,0:T(8,128)(2,1)}), bf16[32,128,128]{2,1,0:T(8,128)(2,1)S(1)}, u32[]{:S(2)}, u32[]{:S(2)}) %all-to-all-start.1) | async-done | bytes 1048608 | tf_op jit(solution)/shard_map/all_to_all | solution.py:189
  241.8 0.0 copy-start.2
  241.8 0.0 all-gather.6.cloned.1.call-done
  241.8 1.0 copy-done.2
  242.8 12.6 %shard_map.66 = bf16[128,5120]{1,0:T(8,128)(2,1)} custom-call(f32[64]{0:T(128)} %reshape.32.mix_ref, bf16[32,128,128]{2,1,0:T(8,128)(2,1)} %copy-done.2, bf16[2,4096,640]{2,1,0:T(8,128)(2,1)} %bitcast.5), custom_call_target="tpu_custom_call" | custom-call | tf_op jit(solution)/shard_map/pallas_call | solution.py:155
  (1 shorter events, 0.0 us)
Async XLA Ops:
  6.5 1.0 copy-start
  6.5 91.3 %all-gather.4.cloned.1.call-start = ((), (), s32[]{:S(2)}) async-start(), calls=%async_computation.2 | async-start | bytes 5406720 | tf_op jit(solution)/shard_map/all_gather | solution.py:177
  8.2 233.6 %all-gather.6.cloned.1.call-start = ((), (), s32[]{:S(2)}) async-start(), calls=%async_computation.3 | async-start | bytes 15728640 | tf_op jit(solution)/shard_map/all_gather | solution.py:178
  102.2 5.7 %copy-start.4 = (s32[3]{0:T(128)S(1)}, s32[3]{0:T(128)}, u32[]{:S(2)}) copy-start(s32[3]{0:T(128)} %param.9) | copy-start | bytes 40
  102.2 77.6 %all-to-all-start = ((bf16[32,3,128,128]{3,2,1,0:T(8,128)(2,1)}), bf16[32,3,128,128]{3,2,1,0:T(8,128)(2,1)S(1)}, u32[]{:S(2)}, u32[]{:S(2)}) async-start(bf16[32,3,128,128]{3,2,1,0:T(8,128)(2,1)} %shard_map.64), calls=%async_computation | async-start | bytes 6291456 | tf_op jit(solution)/shard_map/all_to_all | solution.py:186
  179.8 1.6 copy-start.1
  181.4 31.0 %copy-start.3 = (f32[4,4,4]{2,1,0:T(4,128)S(1)}, f32[4,4,4]{2,1,0:T(4,128)}, u32[]{:S(2)}) copy-start(f32[4,4,4]{2,1,0:T(4,128)} %param.10) | copy-start | bytes 772
  208.4 33.4 %all-to-all-start.1 = ((bf16[32,128,128]{2,1,0:T(8,128)(2,1)}), bf16[32,128,128]{2,1,0:T(8,128)(2,1)S(1)}, u32[]{:S(2)}, u32[]{:S(2)}) async-start(bf16[32,128,128]{2,1,0:T(8,128)(2,1)} %bitcast.6), calls=%async_computation.1 | async-start | bytes 2097152 | tf_op jit(solution)/shard_map/all_to_all | solution.py:189
  241.8 1.0 copy-start.2
Sparse Core Ops, SparseCore 0:
  9.9 87.8 all-gather.3
  99.6 25.0 all-gather.5

commit v7 on v6

--- a/solution.py
+++ b/solution.py
@@ -12,30 +12,34 @@
 HEAD_DIM = 128
 PHM_N = 4
 UNIT = 128
-BQ = 512
+BQ = 1024
+PHASES = 2
 BK = 256
 
 
-def flash_kernel(ends_ref, q_ref, k_ref, v_ref, o_ref):
-    i = pl.program_id(0)
+def flash_kernel(ends_ref, q_ref, k_ref, v_ref, o_ref, *, phase):
+    g = pl.program_id(0)
     e0 = ends_ref[0]
     e1 = ends_ref[1]
     scale = 1.0 / math.sqrt(HEAD_DIM)
     per = BK // UNIT
+    dests, half, _ = q_ref.shape
+    rows = dests * half
 
     def doc_start(t):
         return jnp.where(t >= e1, e1, jnp.where(t >= e0, e0, 0))
 
-    q_lo = i * BQ
-    q_hi = q_lo + BQ - 1
+    q_lo = g * dests * UNIT + phase * half
+    q_hi = q_lo + (dests - 1) * UNIT + half - 1
     j_lo = doc_start(q_lo) // BK
     j_hi = q_hi // BK
     full_lo = (doc_start(q_hi) + BK - 1) // BK
     full_hi = (q_lo + 1) // BK - 1
     mid_lo = jnp.maximum(j_lo, jnp.minimum(full_lo, j_hi + 1))
     mid_hi = jnp.maximum(mid_lo, full_hi + 1)
-    q = q_ref[...].reshape(BQ, HEAD_DIM)
-    q_pos = q_lo + lax.broadcasted_iota(jnp.int32, (BQ, 1), 0)
+    q = q_ref[...].reshape(rows, HEAD_DIM)
+    r = lax.broadcasted_iota(jnp.int32, (rows, 1), 0)
+    q_pos = q_lo + (r // half) * UNIT + r % half
     q_start = doc_start(q_pos)
 
     def step(j, carry, masked):
@@ -61,39 +65,45 @@
         return m_new, l, acc
 
     carry = (
-        jnp.full((BQ, 1), -1e30, jnp.float32),
-        jnp.zeros((BQ, 1), jnp.float32),
-        jnp.zeros((BQ, HEAD_DIM), jnp.float32),
+        jnp.full((rows, 1), -1e30, jnp.float32),
+        jnp.zeros((rows, 1), jnp.float32),
+        jnp.zeros((rows, HEAD_DIM), jnp.float32),
     )
     edge = functools.partial(step, masked=True)
     inner = functools.partial(step, masked=False)
     carry = lax.fori_loop(j_lo, mid_lo, edge, carry)
     carry = lax.fori_loop(mid_lo, mid_hi, inner, carry)
     _, l, acc = lax.fori_loop(mid_hi, j_hi + 1, edge, carry)
-    o_ref[...] = (acc / l).astype(o_ref.dtype)
-
-
-def attend(qkv, ends):
+    o_ref[...] = (acc / l).astype(o_ref.dtype).reshape(dests, half, HEAD_DIM)
+
+
+def attend(qkv, ends, phase):
     blocks = qkv.shape[0]
-    seq = blocks * UNIT
+    half = UNIT // PHASES
+    dests = BQ // UNIT
+    split = qkv.reshape(blocks, 3, PHASES, half, HEAD_DIM)
 
     def whole(which):
-        return pl.BlockSpec((blocks, None, UNIT, HEAD_DIM), lambda i, e: (0, which, 0, 0))
+        return pl.BlockSpec(
+            (blocks, None, PHASES, half, HEAD_DIM), lambda g, e: (0, which, 0, 0, 0)
+        )
 
     return pl.pallas_call(
-        flash_kernel,
+        functools.partial(flash_kernel, phase=phase),
         grid_spec=pltpu.PrefetchScalarGridSpec(
             num_scalar_prefetch=1,
-            grid=(seq // BQ,),
+            grid=(blocks // dests,),
             in_specs=[
-                pl.BlockSpec((BQ // UNIT, None, UNIT, HEAD_DIM), lambda i, e: (i, 0, 0, 0)),
+                pl.BlockSpec(
+                    (dests, None, None, half, HEAD_DIM), lambda g, e: (g, 0, phase, 0, 0)
+                ),
                 whole(1),
                 whole(2),
             ],
-            out_specs=pl.BlockSpec((BQ, HEAD_DIM), lambda i, e: (i, 0)),
+            out_specs=pl.BlockSpec((dests, half, HEAD_DIM), lambda g, e: (g, 0, 0)),
         ),
-        out_shape=jax.ShapeDtypeStruct((seq, HEAD_DIM), jnp.bfloat16),
-    )(ends, qkv, qkv, qkv)
+        out_shape=jax.ShapeDtypeStruct((blocks, half, HEAD_DIM), jnp.bfloat16),
+    )(ends, split, split, split)
 
 
 def pack_kernel(q_ref, k_ref, v_ref, o_ref):
@@ -179,16 +189,15 @@
 
 
 def body(queries, key_rows, value_rows, doc_blocks, phm_mix, phm_blocks):
-    tok_rows = queries.shape[0]
-    heads = queries.shape[1] // HEAD_DIM
     factors = gather_factors(phm_blocks)
     stacked = pack(queries, key_rows, value_rows)
     gathered = lax.all_to_all(stacked, "ctx", split_axis=0, concat_axis=0, tiled=True)
     ends = jnp.cumsum(doc_blocks.astype(jnp.int32) * UNIT).astype(jnp.int32)
-    attended = attend(gathered, ends)
-    returned = lax.all_to_all(
-        attended.reshape(heads, tok_rows, HEAD_DIM), "ctx", split_axis=0, concat_axis=0, tiled=True
-    )
+    returned = []
+    for phase in range(PHASES):
+        attended = attend(gathered, ends, phase)
+        returned.append(lax.all_to_all(attended, "ctx", split_axis=0, concat_axis=0, tiled=True))
+    returned = jnp.concatenate(returned, axis=1)
     return project(returned, phm_mix, factors)
 
 

time: 263 us -> 274 us (1.042)
  the two profiles are of different devices: /device:TPU:2 before, /device:TPU:38 now
where the time goes in v7:
time: 274 us
  waiting for transfers between devices  171 us (62%)
  Pallas kernels  61.7 us (23%)
  starting transfers between devices  22.1 us (8%)
  between operations  13.5 us (5%)
  local copies, waits for them, and re-layouts  3.96 us (1%)
    all_gather x1, waiting for transfers between devices, gather_factors(): over_ctx = lax.all_gather(mine, 'ctx', axis=0, tiled=True)  89.2 us
    all_to_all x1, waiting for transfers between devices, body(): lax.all_to_all(stacked, 'ctx', split_axis=0, concat_axis=0, tiled=True)  68.8 us
    pallas_call x2, Pallas kernels, attend(): pl.pallas_call(functools.partial(flash_kernel, phase=phase), grid_spec=pl...  44.7 us
    all_to_all x2, starting transfers between devices, body(): lax.all_to_all(attended, 'ctx', split_axis=0, concat_axis=0, tiled=True)  16.2 us
    all_to_all x2, waiting for transfers between devices, body(): lax.all_to_all(attended, 'ctx', split_axis=0, concat_axis=0, tiled=True)  12.8 us
    pallas_call x1, Pallas kernels, project(): pl.pallas_call(proj_kernel, grid=(PHM_N,), in_specs=[pl.BlockSpec(memory_...  12.6 us
    all_to_all x1, starting transfers between devices, body(): lax.all_to_all(stacked, 'ctx', split_axis=0, concat_axis=0, tiled=True)  5.92 us
  transfers between devices with their start and end apart: 5, of which 3 were waited for; matrix products, arithmetic and copies ran while one was open for 1% of the time, Pallas kernels for 18%

profile of v7, /device:TPU:38, one launch (start us, length us, event | category | flops | bytes accessed | tf_op | source)
XLA Modules:
  0.0 273.8 jit_solution(3751875532613060809)
XLA Ops:
  6.5 0.0 copy-start
  6.5 0.0 all-gather.4.cloned.1.call-start
  6.5 1.0 copy-done
  7.5 0.7 constant_dynamic-slice_fusion
  8.2 0.0 all-gather.4.cloned.1.call-update
  8.2 0.0 all-gather.6.cloned.1.call-start
  8.3 89.2 %all-gather.4.cloned.1.call-done = bf16[4096,640]{1,0:T(8,128)(2,1)} async-done(((bf16[128,640]{1,0:T(8,128)(2,1)}), bf16[4096,640]{1,0:T(8,128)(2,1)}) %all-gather.4.cloned.1.call-update) | async-done | bytes 5242896 | tf_op jit(solution)/shard_map/all_gather | solution.py:187
  97.4 0.0 all-gather.6.cloned.1.call-update
  97.5 4.4 %shard_map.64 = bf16[32,3,128,128]{3,2,1,0:T(8,128)(2,1)} custom-call(bf16[128,4096]{1,0:T(8,128)(2,1)} %q_ref.1, bf16[128,4096]{1,0:T(8,128)(2,1)} %k_ref.1, bf16[128,4096]{1,0:T(8,128)(2,1)} %v_ref.1), custom_call_target="tpu_custom_call" | custom-call | tf_op jit(solution)/shard_map/pallas_call | solution.py:121
  101.8 0.0 copy-start.3
  101.8 5.9 %all-to-all-start = ((bf16[32,3,128,128]{3,2,1,0:T(8,128)(2,1)}), bf16[32,3,128,128]{3,2,1,0:T(8,128)(2,1)S(1)}, u32[]{:S(2)}, u32[]{:S(2)}) async-start(bf16[32,3,128,128]{3,2,1,0:T(8,128)(2,1)} %shard_map.64), calls=%async_computation | async-start | bytes 6291456 | tf_op jit(solution)/shard_map/all_to_all | solution.py:194
  107.8 0.0 copy-done.3
  107.8 0.7 reduce-window.9
  108.5 68.8 %all-to-all-done = bf16[32,3,128,128]{3,2,1,0:T(8,128)(2,1)S(1)} async-done(((bf16[32,3,128,128]{3,2,1,0:T(8,128)(2,1)}), bf16[32,3,128,128]{3,2,1,0:T(8,128)(2,1)S(1)}, u32[]{:S(2)}, u32[]{:S(2)}) %all-to-all-start) | async-done | bytes 3145760 | tf_op jit(solution)/shard_map/all_to_all | solution.py:194
  177.3 0.0 copy-start.1
  177.3 1.6 copy-done.1
  178.9 22.3 %shard_map.66 = bf16[32,64,128]{2,1,0:T(8,128)(2,1)} custom-call(s32[3]{0:T(128)} %bitcast.12, bf16[32,3,2,64,128]{4,3,2,1,0:T(8,128)(2,1)} %bitcast.5, bf16[32,3,2,64,128]{4,3,2,1,0:T(8,128)(2,1)} %bitcast.6, bf16[32,3,2,64,128]{4,3,2,1,0:T(8,128)(2,1)} %bitcast.7), custom_call_target="tpu_custom_call" | custom-call | tf_op jit(solution)/shard_map/pallas_call | solution.py:91
  201.2 6.4 %all-to-all-start.2 = ((bf16[32,64,128]{2,1,0:T(8,128)(2,1)}), bf16[32,64,128]{2,1,0:T(8,128)(2,1)S(1)}, u32[]{:S(2)}, u32[]{:S(2)}) async-start(bf16[32,64,128]{2,1,0:T(8,128)(2,1)} %shard_map.66), calls=%async_computation.2 | async-start | bytes 1048576 | tf_op jit(solution)/shard_map/all_to_all | solution.py:199
  207.6 0.0 copy-start.2
  207.6 22.4 %shard_map.65 = bf16[32,64,128]{2,1,0:T(8,128)(2,1)} custom-call(s32[3]{0:T(128)} %bitcast.13, bf16[32,3,2,64,128]{4,3,2,1,0:T(8,128)(2,1)} %bitcast.8, bf16[32,3,2,64,128]{4,3,2,1,0:T(8,128)(2,1)} %bitcast.9, bf16[32,3,2,64,128]{4,3,2,1,0:T(8,128)(2,1)} %bitcast.10), custom_call_target="tpu_custom_call" | custom-call | tf_op jit(solution)/shard_map/pallas_call | solution.py:91
  230.0 0.0 all-to-all-done.2
  230.0 9.8 %all-to-all-start.1 = ((bf16[32,64,128]{2,1,0:T(8,128)(2,1)}), bf16[32,64,128]{2,1,0:T(8,128)(2,1)S(1)}, u32[]{:S(2)}, u32[]{:S(2)}) async-start(bf16[32,64,128]{2,1,0:T(8,128)(2,1)} %shard_map.65), calls=%async_computation.1 | async-start | bytes 1048576 | tf_op jit(solution)/shard_map/all_to_all | solution.py:199
  239.8 0.0 copy-done.2
  239.8 0.7 reshape.33.mix_ref
  240.5 12.8 %all-to-all-done.1 = bf16[32,64,128]{2,1,0:T(8,128)(2,1)S(1)} async-done(((bf16[32,64,128]{2,1,0:T(8,128)(2,1)}), bf16[32,64,128]{2,1,0:T(8,128)(2,1)S(1)}, u32[]{:S(2)}, u32[]{:S(2)}) %all-to-all-start.1) | async-done | bytes 524320 | tf_op jit(solution)/shard_map/all_to_all | solution.py:199
  253.3 1.1 pad_maximum_fusion.att_ref
  254.3 0.0 all-gather.6.cloned.1.call-done
  254.3 12.6 %shard_map.67 = bf16[128,5120]{1,0:T(8,128)(2,1)} custom-call(f32[64]{0:T(128)} %reshape.33.mix_ref, bf16[32,128,128]{2,1,0:T(8,128)(2,1)} %pad_maximum_fusion.att_ref, bf16[2,4096,640]{2,1,0:T(8,128)(2,1)} %bitcast.11), custom_call_target="tpu_custom_call" | custom-call | tf_op jit(solution)/shard_map/pallas_call | solution.py:165
  (1 shorter events, 0.0 us)
Async XLA Ops:
  6.5 1.0 copy-start
  6.5 90.9 %all-gather.4.cloned.1.call-start = ((), (), s32[]{:S(2)}) async-start(), calls=%async_computation.3 | async-start | bytes 5406720 | tf_op jit(solution)/shard_map/all_gather | solution.py:187
  8.2 246.1 %all-gather.6.cloned.1.call-start = ((), (), s32[]{:S(2)}) async-start(), calls=%async_computation.4 | async-start | bytes 15728640 | tf_op jit(solution)/shard_map/all_gather | solution.py:188
  101.8 5.9 %copy-start.3 = (s32[3]{0:T(128)S(1)}, s32[3]{0:T(128)}, u32[]{:S(2)}) copy-start(s32[3]{0:T(128)} %param.9) | copy-start | bytes 40
  101.8 75.4 %all-to-all-start = ((bf16[32,3,128,128]{3,2,1,0:T(8,128)(2,1)}), bf16[32,3,128,128]{3,2,1,0:T(8,128)(2,1)S(1)}, u32[]{:S(2)}, u32[]{:S(2)}) async-start(bf16[32,3,128,128]{3,2,1,0:T(8,128)(2,1)} %shard_map.64), calls=%async_computation | async-start | bytes 6291456 | tf_op jit(solution)/shard_map/all_to_all | solution.py:194
  177.3 1.6 copy-start.1
  201.2 28.9 %all-to-all-start.2 = ((bf16[32,64,128]{2,1,0:T(8,128)(2,1)}), bf16[32,64,128]{2,1,0:T(8,128)(2,1)S(1)}, u32[]{:S(2)}, u32[]{:S(2)}) async-start(bf16[32,64,128]{2,1,0:T(8,128)(2,1)} %shard_map.66), calls=%async_computation.2 | async-start | bytes 1048576 | tf_op jit(solution)/shard_map/all_to_all | solution.py:199
  207.6 32.2 %copy-start.2 = (f32[4,4,4]{2,1,0:T(4,128)S(1)}, f32[4,4,4]{2,1,0:T(4,128)}, u32[]{:S(2)}) copy-start(f32[4,4,4]{2,1,0:T(4,128)} %param.10) | copy-start | bytes 772
  230.0 23.2 %all-to-all-start.1 = ((bf16[32,64,128]{2,1,0:T(8,128)(2,1)}), bf16[32,64,128]{2,1,0:T(8,128)(2,1)S(1)}, u32[]{:S(2)}, u32[]{:S(2)}) async-start(bf16[32,64,128]{2,1,0:T(8,128)(2,1)} %shard_map.65), calls=%async_computation.1 | async-start | bytes 1048576 | tf_op jit(solution)/shard_map/all_to_all | solution.py:199
Sparse Core Ops, SparseCore 0:
  9.9 87.4 all-gather.3
  99.2 24.9 all-gather.5
